TPU v7x, 32 devices: a whole 2x2x4 slice. The times are simulated.
32 devices in a mesh: row: 16 (over z, x, core), col: 2 (over y).
Axes of the slice: x: 2, y: 2, z: 4, core: 2. Of those that a mesh axis runs over, the one named last changes fastest.
Arguments:
- counts: int32 [3072, 3072], P('row', 'col'), may hold values from 0 to 3
- theta: bfloat16 [3072, 64], P(('row', 'col')), may hold values from 0.099609375 to 1
- phi: bfloat16 [3072, 64], P(('col', 'row')), may hold values from 0.099609375 to 1
- affinity: float32 [64, 64], replicated, may hold values from 0.0003 to 0.003
Outputs:
- theta_grad: float32 [3072, 64], P(('row', 'col'))
- phi_grad: float32 [3072, 64], P(('col', 'row'))
- affinity_grad: float32 [64, 64], replicated
All inputs are finite; a program needn't handle non-finite values.
Results may differ from a plain program's by a relative error of at most 0.0003.
Values may be sent and summed in bfloat16 or wider, within the bound.
No kernel may reach another device: no remote copies, remote signals or barrier semaphores. Data moves between devices by JAX's collectives and lax.ppermute only.
A program may use at most 64 MiB of HBM per device.

v0:
```python
import jax
import jax.numpy as jnp
from jax import lax
from jax.sharding import PartitionSpec as P


def shards(counts, theta, phi, affinity):
    nodes = theta.shape[0] * lax.axis_size("row") * lax.axis_size("col")
    inverse = 1.0 / nodes
    theta_rows = lax.all_gather(theta, "col", axis=0, tiled=True)
    row_factor = jnp.dot(theta_rows.astype(jnp.float32), affinity, precision=lax.Precision.HIGHEST)
    factor_half = row_factor.astype(jnp.bfloat16)
    members = lax.all_gather(phi, "row", axis=0, tiled=True)
    rate = jnp.dot(row_factor, members.astype(jnp.float32).T, precision=lax.Precision.HIGHEST)
    ratio = (1.0 - counts.astype(jnp.float32) / rate).astype(jnp.bfloat16)
    gphi = jnp.dot(ratio, members, preferred_element_type=jnp.float32)
    phi_sum = lax.psum_scatter(
        lax.dot_general(
            ratio, factor_half, (((0,), (0,)), ((), ())), preferred_element_type=jnp.float32
        ),
        "row",
        scatter_dimension=0,
        tiled=True,
    )
    gphi_sum = lax.psum_scatter(gphi, "col", scatter_dimension=0, tiled=True)
    theta_grad = inverse * jnp.dot(gphi_sum, affinity.T, precision=lax.Precision.HIGHEST)
    phi_grad = inverse * phi_sum
    affinity_part = jnp.dot(theta.astype(jnp.float32).T, gphi_sum, precision=lax.Precision.HIGHEST)
    affinity_grad = inverse * inverse * lax.psum(affinity_part, ("row", "col"))
    return (theta_grad, phi_grad, affinity_grad)


def solution(mesh):
    placed = (P("row", "col"), P(("row", "col"), None), P(("col", "row"), None), P())
    return jax.shard_map(
        shards,
        mesh=mesh,
        in_specs=placed,
        out_specs=(P(("row", "col"), None), P(("col", "row"), None), P()),
        check_vma=False,
    )
```

profile of v0, /device:TPU:0, one launch (start us, length us, event | category | flops | bytes accessed | tf_op | source)
XLA Modules:
  0.0 114.5 jit_solution(16224483972441247521)
XLA Ops:
  7.2 0.0 copy-start
  7.2 0.0 copy-start.2
  7.2 0.0 reduce-scatter.7.cloned.1.call-start
  7.2 5.7 %all-gather = bf16[2,96,64]{1,2,0:T(8,128)(2,1)S(1)} all-gather(bf16[1,96,64]{1,2,0:T(8,128)(2,1)} %bitcast.21), channel_id=1, replica_groups=mesh['row'=16,'col'=2] {'col'}, dimensions={0}, use_global_device_ids=true | all-gather | bytes 36864 | tf_op jit(solution)/shard_map/all_gather | solution.py:10
  13.0 0.1 reshape.7
  13.1 23.0 %all-gather.1 = bf16[16,96,64]{1,2,0:T(8,128)(2,1)S(1)} all-gather(bf16[1,96,64]{1,2,0:T(8,128)(2,1)} %bitcast.22), channel_id=1, replica_groups=mesh['row'=16,'col'=2] {'row'}, dimensions={0}, use_global_device_ids=true | all-gather | bytes 208896 | tf_op jit(solution)/shard_map/all_gather | solution.py:13
  36.2 0.2 copy.12
  36.3 0.3 reshape.9
  36.6 0.0 copy-done
  36.6 0.2 fusion.4
  36.8 0.0 copy-done.2
  36.8 0.7 fusion.1
  37.6 0.9 fusion.5
  38.5 0.0 copy-start.1
  38.5 0.0 reduce-scatter.7.cloned.1.call-update
  38.6 0.0 reduce-scatter.9.cloned.1.call-start
  38.6 1.3 %fusion.2 = f32[1536,64]{1,0:T(8,128)} fusion(bf16[192,1536]{1,0:T(8,128)(2,1)S(1)} %fusion.1, f32[192,64]{0,1:T(8,128)S(1)} %fusion.4), kind=kOutput, calls=%fused_computation.5 | convolution fusion | flops 37761024 | bytes 1032192
  39.9 0.0 reduce-scatter.9.cloned.1.call-update
  40.0 6.1 %reduce-scatter.7.cloned.1.call-done = f32[96,64]{1,0:T(8,128)} async-done(((f32[192,64]{1,0:T(8,128)}), f32[96,64]{1,0:T(8,128)}) %reduce-scatter.7.cloned.1.call-update) | async-done | bytes 24592
  46.0 0.0 copy-done.1
  46.0 1.0 convolution_bitcast_fusion
  47.0 39.5 %psum.7 = f32[64,64]{0,1:T(8,128)S(1)} all-reduce(f32[64,64]{0,1:T(8,128)S(1)} %convolution_bitcast_fusion), channel_id=1, replica_groups=mesh['row'=16,'col'=2] {'row','col'}, use_global_device_ids=true, to_apply=%region_2.0 | all-reduce | flops 4096 | bytes 32768 | tf_op jit(solution)/shard_map/psum | solution.py:29
  86.6 0.7 copy.13
  87.3 1.6 %convolution_multiply_fusion = f32[96,64]{0,1:T(8,128)} fusion(f32[96,64]{1,0:T(8,128)} %reduce-scatter.7.cloned.1.call-done, f32[64,64]{1,0:T(8,128)S(1)} %copy-done), kind=kOutput, calls=%fused_computation.4 | convolution fusion | flops 4724736 | bytes 65536 | tf_op jit(solution)/shard_map/dot_general | solution.py:26
  88.9 17.3 %reduce-scatter.9.cloned.1.call-done = f32[96,64]{1,0:T(8,128)} async-done(((f32[1536,64]{1,0:T(8,128)}), f32[96,64]{1,0:T(8,128)}) %reduce-scatter.9.cloned.1.call-update) | async-done | bytes 24592
  106.2 0.9 copy.17
  107.0 0.6 broadcast_multiply_fusion.1
  (2 shorter events, 0.0 us)
Async XLA Ops:
  7.2 29.4 %copy-start = (f32[64,64]{1,0:T(8,128)S(1)}, f32[64,64]{1,0:T(8,128)}, u32[]{:S(2)}) copy-start(f32[64,64]{1,0:T(8,128)} %param.7) | copy-start | bytes 49156
  7.2 29.7 %copy-start.2 = (s32[192,1536]{1,0:T(8,128)S(1)}, s32[192,1536]{1,0:T(8,128)}, u32[]{:S(2)}) copy-start(s32[192,1536]{1,0:T(8,128)} %param.4) | copy-start | bytes 3538948
  7.2 38.8 %reduce-scatter.7.cloned.1.call-start = ((), (), s32[]{:S(2)}) async-start(), calls=%async_computation.2 | async-start | bytes 147456
  38.5 7.5 %copy-start.1 = (bf16[96,64]{0,1:T(8,128)(2,1)S(1)}, bf16[96,64]{0,1:T(8,128)(2,1)}, u32[]{:S(2)}) copy-start(bf16[96,64]{0,1:T(8,128)(2,1)} %param.5) | copy-start | bytes 36868
  38.6 67.6 %reduce-scatter.9.cloned.1.call-start = ((), (), s32[]{:S(2)}) async-start(), calls=%async_computation.3 | async-start | bytes 835584
Sparse Core Ops, SparseCore 0:
  38.7 7.2 reduce-scatter.6
  49.6 56.5 reduce-scatter.8
where the time goes:
time: 115 us; the launch traced here: 114 us
  blocking collectives  68.3 us (59%)
  waiting for transfers between devices  23.3 us (20%)
  between operations  14.1 us (12%)
  matrix products  5.89 us (5%)
  local copies, waits for them, and re-layouts  2.15 us (2%)
    psum x1, blocking collectives, shards(): affinity_grad = inverse * inverse * lax.psum(affinity_part, ('row', 'col'))  39.5 us
    unnamed x4, waiting for transfers between devices  23.3 us
    all_gather x1, blocking collectives, shards(): members = lax.all_gather(phi, 'row', axis=0, tiled=True)  23 us
    all_gather x1, blocking collectives, shards(): theta_rows = lax.all_gather(theta, 'col', axis=0, tiled=True)  5.75 us
  transfers between devices with their start and end apart: 2, of which 2 were waited for; matrix products, arithmetic and copies ran while one was open for 4% of the time, Pallas kernels for 0%

commit v1 on v0

v1 whole, which is shorter than its diff:
```python
import jax
import jax.numpy as jnp
from jax import lax
from jax.sharding import PartitionSpec as P

HI = lax.Precision.HIGHEST


def gather_rows(x, axis):
    n = lax.axis_size(axis)
    slots = jnp.broadcast_to(x[None], (n,) + x.shape)
    got = lax.all_to_all(slots, axis, 0, 0)
    return got.reshape((n * x.shape[0],) + x.shape[1:])


def shards(counts, theta, phi, affinity):
    nr, nc = lax.axis_size("row"), lax.axis_size("col")
    nodes = theta.shape[0] * nr * nc
    inverse = 1.0 / nodes
    k = theta.shape[1]
    c = lax.axis_index("col")
    if nc == 2:
        other = lax.ppermute(theta, "col", [(0, 1), (1, 0)])
        theta_rows = jnp.where(c == 0, jnp.concatenate([theta, other]), jnp.concatenate([other, theta]))
    else:
        theta_rows = gather_rows(theta, "col")
    members = gather_rows(phi, "row")
    theta_wide = theta_rows.astype(jnp.float32)
    row_factor = jnp.dot(theta_wide, affinity, precision=HI)
    factor_half = row_factor.astype(jnp.bfloat16)
    rate = jnp.dot(row_factor, members.astype(jnp.float32).T, precision=HI)
    ratio = (1.0 - counts.astype(jnp.float32) / rate).astype(jnp.bfloat16)
    gphi = jnp.dot(ratio, members, preferred_element_type=jnp.float32)
    gcol = lax.dot_general(ratio, factor_half, (((0,), (0,)), ((), ())), preferred_element_type=jnp.float32)
    part = jnp.dot(theta_wide.T, gphi, precision=HI)
    mc = gphi.shape[0] // nc
    if nc == 2:
        send = jnp.concatenate([lax.dynamic_slice_in_dim(gphi, (1 - c) * mc, mc), part])
        got = lax.ppermute(send, "col", [(0, 1), (1, 0)])
        gphi_sum = lax.dynamic_slice_in_dim(gphi, c * mc, mc) + got[:mc]
        part_col = part + got[mc:]
    else:
        slots = jnp.concatenate([gphi.reshape(nc, mc, k), jnp.broadcast_to(part[None], (nc, k, k))], axis=1)
        got = lax.all_to_all(slots, "col", 0, 0)
        gphi_sum = jnp.sum(got[:, :mc], axis=0)
        part_col = jnp.sum(got[:, mc:], axis=0)
    mr = gcol.shape[0] // nr
    slots = jnp.concatenate([gcol.reshape(nr, mr, k), jnp.broadcast_to(part_col[None], (nr, k, k))], axis=1)
    got = lax.all_to_all(slots, "row", 0, 0)
    phi_sum = jnp.sum(got[:, :mr], axis=0)
    part_all = jnp.sum(got[:, mr:], axis=0)
    theta_grad = inverse * jnp.dot(gphi_sum, affinity.T, precision=HI)
    phi_grad = inverse * phi_sum
    affinity_grad = inverse * inverse * part_all
    return (theta_grad, phi_grad, affinity_grad)


def solution(mesh):
    placed = (P("row", "col"), P(("row", "col"), None), P(("col", "row"), None), P())
    return jax.shard_map(
        shards,
        mesh=mesh,
        in_specs=placed,
        out_specs=(P(("row", "col"), None), P(("col", "row"), None), P()),
        check_vma=False,
    )
```

time: 115 us -> 57.2 us (0.50)
  the two profiles are of different devices: /device:TPU:0 before, /device:TPU:11 now
where the time goes in v1:
time: 57.2 us; the launch traced here: 56.6 us
  waiting for transfers between devices  31.3 us (55%)
  starting transfers between devices  15.5 us (27%)
  matrix products  3.41 us (6%)
  local copies, waits for them, and re-layouts  3.18 us (6%)
  other arithmetic  2.33 us (4%)
  between operations  0.76 us (1%)
    all_to_all x1, waiting for transfers between devices, shards(): got = lax.all_to_all(slots, 'row', 0, 0)  24 us
    all_to_all x1, starting transfers between devices, gather_rows(): got = lax.all_to_all(slots, axis, 0, 0)  6.55 us
    all_to_all x1, starting transfers between devices, shards(): got = lax.all_to_all(slots, 'row', 0, 0)  6.45 us
    all_to_all x1, waiting for transfers between devices, gather_rows(): got = lax.all_to_all(slots, axis, 0, 0)  4.09 us
    ppermute x1, waiting for transfers between devices, shards(): got = lax.ppermute(send, 'col', [(0, 1), (1, 0)])  1.66 us
    ppermute x1, waiting for transfers between devices, shards(): other = lax.ppermute(theta, 'col', [(0, 1), (1, 0)])  1.56 us
    broadcast_in_dim x1, local copies, waits for them, and re-layouts, gather_rows(): slots = jnp.broadcast_to(x[None], (n,) + x.shape)  1.56 us
    concatenate x1, other arithmetic, shards(): jnp.concatenate([gcol.reshape(nr, mr, k), jnp.broadcast_to(part_col[None]...  1.31 us
  transfers between devices with their start and end apart: 4, of which 4 were waited for; matrix products, arithmetic and copies ran while one was open for 4% of the time, Pallas kernels for 0%

profile of v1, /device:TPU:11, one launch (start us, length us, event | category | flops | bytes accessed | tf_op | source)
XLA Modules:
  0.0 56.6 jit_solution(13373749044101295187)
XLA Ops:
  0.6 0.0 copy-start
  0.6 0.0 copy-start.2
  0.7 1.6 %broadcast_in_dim.4 = bf16[16,96,64]{1,2,0:T(8,128)(2,1)} broadcast(bf16[96,64]{0,1:T(8,128)(2,1)} %param.6), dimensions={1,2} | broadcast | bytes 208896 | tf_op jit(solution)/shard_map/broadcast_in_dim | solution.py:11
  2.2 6.6 %all-to-all-start = ((bf16[16,96,64]{1,2,0:T(8,128)(2,1)}), bf16[16,96,64]{1,2,0:T(8,128)(2,1)S(1)}, u32[]{:S(2)}, u32[]{:S(2)}) async-start(bf16[16,96,64]{1,2,0:T(8,128)(2,1)} %broadcast_in_dim.4), calls=%async_computation | async-start | bytes 524288 | tf_op jit(solution)/shard_map/all_to_all | solution.py:12
  8.8 1.2 %collective-permute-start = (bf16[96,64]{0,1:T(8,128)(2,1)}, bf16[96,64]{0,1:T(8,128)(2,1)S(1)}, u32[]{:S(2)}, u32[]{:S(2)}) collective-permute-start(bf16[96,64]{0,1:T(8,128)(2,1)} %param.5), channel_id=1, source_target_pairs={{0,1},{1,0},{2,3},{3,2},{4,5},{5,4},{6,7},{7,6},{8,9},{9,8},{10,11... | collective-permute-start | bytes 36872 | tf_op jit(solution)/shard_map/ppermute | solution.py:23
  10.0 1.6 %collective-permute-done = bf16[96,64]{0,1:T(8,128)(2,1)S(1)} collective-permute-done((bf16[96,64]{0,1:T(8,128)(2,1)}, bf16[96,64]{0,1:T(8,128)(2,1)S(1)}, u32[]{:S(2)}, u32[]{:S(2)}) %collective-permute-start) | collective-permute-done | bytes 12320 | tf_op jit(solution)/shard_map/ppermute | solution.py:23
  11.6 0.0 copy-done
  11.6 1.1 %fusion.6 = f32[192,64]{0,1:T(8,128)S(1)} fusion(f32[64,64]{1,0:T(8,128)S(1)} %copy-done, bf16[96,64]{0,1:T(8,128)(2,1)S(1)} %collective-permute-done, bf16[96,64]{0,1:T(8,128)(2,1)} %param.5, pred[]{:T(512)S(6)} %eq.3), kind=kOutput, calls=%fused_computation.17 | convolution fusion | flops 9547776 | bytes 90113 | tf_op jit(solution)/shard_map/dot_general | solution.py:29
  12.6 4.1 %all-to-all-done = bf16[16,96,64]{1,2,0:T(8,128)(2,1)S(1)} async-done(((bf16[16,96,64]{1,2,0:T(8,128)(2,1)}), bf16[16,96,64]{1,2,0:T(8,128)(2,1)S(1)}, u32[]{:S(2)}, u32[]{:S(2)}) %all-to-all-start) | async-done | bytes 196640 | tf_op jit(solution)/shard_map/all_to_all | solution.py:12
  16.7 0.2 copy.11
  16.9 0.3 reshape.14
  17.2 0.0 copy-done.2
  17.2 0.0 copy-start.1
  17.2 0.7 %fusion.1 = bf16[192,1536]{1,0:T(8,128)(2,1)S(1)} fusion(f32[192,64]{0,1:T(8,128)S(1)} %fusion.6, bf16[1536,64]{0,1:T(8,128)(2,1)S(1)} %reshape.14, s32[192,1536]{1,0:T(8,128)S(1)} %copy-done.2), kind=kOutput, calls=%fused_computation.2 | convolution fusion | flops 227672064 | bytes 2015232 | tf_op jit(solution)/shard_map/dot_general | solution.py:31
  17.9 0.3 fusion.10
  18.2 0.1 constant_dynamic-slice_fusion
  18.3 0.0 copy-done.1
  18.3 0.3 fusion.5
  18.6 0.1 pad_maximum_fusion.1
  18.7 1.3 %collective-permute-start.1 = (f32[160,64]{0,1:T(8,128)S(1)}, f32[160,64]{0,1:T(8,128)S(1)}, u32[]{:S(2)}, u32[]{:S(2)}) collective-permute-start(f32[160,64]{0,1:T(8,128)S(1)} %pad_maximum_fusion.1), channel_id=1, source_target_pairs={{0,1},{1,0},{2,3},{3,2},{4,5},{5,4},{6,7},{7,6},{8,9},{9,8},{10,11... | collective-permute-start | bytes 122888 | tf_op jit(solution)/shard_map/ppermute | solution.py:39
  20.0 0.2 fusion.2
  20.2 0.2 reshape.15
  20.4 0.2 copy.12
  20.6 1.7 %collective-permute-done.1 = f32[160,64]{0,1:T(8,128)S(1)} collective-permute-done((f32[160,64]{0,1:T(8,128)S(1)}, f32[160,64]{0,1:T(8,128)S(1)}, u32[]{:S(2)}, u32[]{:S(2)}) %collective-permute-start.1) | collective-permute-done | bytes 40992 | tf_op jit(solution)/shard_map/ppermute | solution.py:39
  22.2 0.1 slice_add_fusion
  22.3 1.3 %pad_maximum_fusion = f32[16,160,64]{1,2,0:T(8,128)} fusion(f32[16,64,64]{1,2,0:T(8,128)S(1)} %broadcast_in_dim.5, f32[16,96,64]{1,2,0:T(8,128)S(1)} %copy.12), kind=kLoop, calls=%fused_computation.4 | loop fusion | flops 163840 | bytes 1310720 | tf_op jit(solution)/shard_map/concatenate | solution.py:48
  23.7 6.4 %all-to-all-start.1 = ((f32[16,160,64]{1,2,0:T(8,128)}), f32[16,160,64]{1,2,0:T(8,128)S(1)}, u32[]{:S(2)}, u32[]{:S(2)}) async-start(f32[16,160,64]{1,2,0:T(8,128)} %pad_maximum_fusion), calls=%async_computation.1 | async-start | bytes 2097152 | tf_op jit(solution)/shard_map/all_to_all | solution.py:49
  30.1 0.9 %convolution_multiply_fusion = f32[96,64]{0,1:T(8,128)} fusion(f32[64,64]{1,0:T(8,128)S(1)} %copy-done, f32[160,64]{0,1:T(8,128)S(1)} %collective-permute-done.1, f32[192,64]{0,1:T(8,128)S(1)} %fusion.10, s32[]{:T(128)S(6)} %select_n.16), kind=kOutput, calls=%fused_computation.3 | convolution fusion | flops 4730880 | bytes 122884 | tf_op jit(solution)/shard_map/dot_general | solution.py:52
  31.0 24.0 %all-to-all-done.1 = f32[16,160,64]{1,2,0:T(8,128)S(1)} async-done(((f32[16,160,64]{1,2,0:T(8,128)}), f32[16,160,64]{1,2,0:T(8,128)S(1)}, u32[]{:S(2)}, u32[]{:S(2)}) %all-to-all-start.1) | async-done | bytes 655392 | tf_op jit(solution)/shard_map/all_to_all | solution.py:49
  55.1 0.6 %broadcast_multiply_fusion.1 = f32[96,64]{0,1:T(8,128)} fusion(f32[96,64]{0,1:T(8,128)S(1)} %slice_reduce_fusion.1), kind=kLoop, calls=%fused_computation.15 | loop fusion | flops 6144 | bytes 49152 | tf_op jit(solution)/shard_map/mul | solution.py:53
  55.7 0.2 slice_reduce_fusion
  55.9 0.7 %copy.14 = f32[64,64]{1,0:T(8,128)} copy(f32[64,64]{0,1:T(8,128)S(1)} %broadcast_multiply_fusion) | data formatting | bytes 32768
  (3 shorter events, 0.1 us)
Async XLA Ops:
  0.6 10.9 %copy-start = (f32[64,64]{1,0:T(8,128)S(1)}, f32[64,64]{1,0:T(8,128)}, u32[]{:S(2)}) copy-start(f32[64,64]{1,0:T(8,128)} %param.7) | copy-start | bytes 49156
  0.6 16.5 %copy-start.2 = (s32[192,1536]{1,0:T(8,128)S(1)}, s32[192,1536]{1,0:T(8,128)}, u32[]{:S(2)}) copy-start(s32[192,1536]{1,0:T(8,128)} %param.4) | copy-start | bytes 3538948
  2.2 14.5 %all-to-all-start = ((bf16[16,96,64]{1,2,0:T(8,128)(2,1)}), bf16[16,96,64]{1,2,0:T(8,128)(2,1)S(1)}, u32[]{:S(2)}, u32[]{:S(2)}) async-start(bf16[16,96,64]{1,2,0:T(8,128)(2,1)} %broadcast_in_dim.4), calls=%async_computation | async-start | bytes 524288 | tf_op jit(solution)/shard_map/all_to_all | solution.py:12
  8.8 2.8 %collective-permute-start = (bf16[96,64]{0,1:T(8,128)(2,1)}, bf16[96,64]{0,1:T(8,128)(2,1)S(1)}, u32[]{:S(2)}, u32[]{:S(2)}) collective-permute-start(bf16[96,64]{0,1:T(8,128)(2,1)} %param.5), channel_id=1, source_target_pairs={{0,1},{1,0},{2,3},{3,2},{4,5},{5,4},{6,7},{7,6},{8,9},{9,8},{10,11... | collective-permute-start | bytes 36872 | tf_op jit(solution)/shard_map/ppermute | solution.py:23
  17.2 1.1 %copy-start.1 = (bf16[96,64]{0,1:T(8,128)(2,1)S(1)}, bf16[96,64]{0,1:T(8,128)(2,1)}, u32[]{:S(2)}) copy-start(bf16[96,64]{0,1:T(8,128)(2,1)} %param.5) | copy-start | bytes 36868
  18.7 3.5 %collective-permute-start.1 = (f32[160,64]{0,1:T(8,128)S(1)}, f32[160,64]{0,1:T(8,128)S(1)}, u32[]{:S(2)}, u32[]{:S(2)}) collective-permute-start(f32[160,64]{0,1:T(8,128)S(1)} %pad_maximum_fusion.1), channel_id=1, source_target_pairs={{0,1},{1,0},{2,3},{3,2},{4,5},{5,4},{6,7},{7,6},{8,9},{9,8},{10,11... | collective-permute-start | bytes 122888 | tf_op jit(solution)/shard_map/ppermute | solution.py:39
  23.7 31.3 %all-to-all-start.1 = ((f32[16,160,64]{1,2,0:T(8,128)}), f32[16,160,64]{1,2,0:T(8,128)S(1)}, u32[]{:S(2)}, u32[]{:S(2)}) async-start(f32[16,160,64]{1,2,0:T(8,128)} %pad_maximum_fusion), calls=%async_computation.1 | async-start | bytes 2097152 | tf_op jit(solution)/shard_map/all_to_all | solution.py:49

commit v2 on v1

--- a/solution.py
+++ b/solution.py
@@ -45,10 +45,13 @@
         gphi_sum = jnp.sum(got[:, :mc], axis=0)
         part_col = jnp.sum(got[:, mc:], axis=0)
     mr = gcol.shape[0] // nr
-    slots = jnp.concatenate([gcol.reshape(nr, mr, k), jnp.broadcast_to(part_col[None], (nr, k, k))], axis=1)
-    got = lax.all_to_all(slots, "row", 0, 0)
-    phi_sum = jnp.sum(got[:, :mr], axis=0)
-    part_all = jnp.sum(got[:, mr:], axis=0)
+    got = lax.all_to_all(gcol.reshape(nr, mr, k), "row", 0, 0)
+    phi_sum = jnp.sum(got, axis=0)
+    part_all = part_col
+    step = 1
+    while step < nr:
+        part_all = part_all + lax.ppermute(part_all, "row", [(i, i ^ step) for i in range(nr)])
+        step *= 2
     theta_grad = inverse * jnp.dot(gphi_sum, affinity.T, precision=HI)
     phi_grad = inverse * phi_sum
     affinity_grad = inverse * inverse * part_all

time: 57.2 us -> 46.7 us (0.82)
  the two profiles are of different devices: /device:TPU:11 before, /device:TPU:0 now
where the time goes in v2:
time: 46.7 us; the launch traced here: 46.1 us
  starting transfers between devices  20.8 us (45%)
  waiting for transfers between devices  16.3 us (35%)
  local copies, waits for them, and re-layouts  3.94 us (8%)
  matrix products  3.42 us (7%)
  other arithmetic  0.85 us (2%)
  between operations  0.76 us (2%)
    ppermute x4, waiting for transfers between devices, shards(): lax.ppermute(part_all, 'row', [(i, i ^ step) for i in range(nr)])  8.92 us
    all_to_all x1, starting transfers between devices, gather_rows(): got = lax.all_to_all(slots, axis, 0, 0)  7.36 us
    ppermute x4, starting transfers between devices, shards(): lax.ppermute(part_all, 'row', [(i, i ^ step) for i in range(nr)])  6.7 us
    all_to_all x1, waiting for transfers between devices, gather_rows(): got = lax.all_to_all(slots, axis, 0, 0)  4.97 us
    all_to_all x1, starting transfers between devices, shards(): got = lax.all_to_all(gcol.reshape(nr, mr, k), 'row', 0, 0)  3.57 us
    ppermute x1, waiting for transfers between devices, shards(): other = lax.ppermute(theta, 'col', [(0, 1), (1, 0)])  2.43 us
    ppermute x1, starting transfers between devices, shards(): other = lax.ppermute(theta, 'col', [(0, 1), (1, 0)])  1.58 us
    ppermute x1, starting transfers between devices, shards(): got = lax.ppermute(send, 'col', [(0, 1), (1, 0)])  1.58 us
  transfers between devices with their start and end apart: 8, of which 6 were waited for; matrix products, arithmetic and copies ran while one was open for 9% of the time, Pallas kernels for 0%

profile of v2, /device:TPU:0, one launch (start us, length us, event | category | flops | bytes accessed | tf_op | source)
XLA Modules:
  0.0 46.1 jit_solution(14808600350419242702)
XLA Ops:
  0.6 0.0 copy-start
  0.6 0.0 copy-start.2
  0.7 1.6 %broadcast_in_dim.2 = bf16[16,96,64]{1,2,0:T(8,128)(2,1)} broadcast(bf16[96,64]{0,1:T(8,128)(2,1)} %param.6), dimensions={1,2} | broadcast | bytes 208896 | tf_op jit(solution)/shard_map/broadcast_in_dim | solution.py:11
  2.2 7.4 %all-to-all-start = ((bf16[16,96,64]{1,2,0:T(8,128)(2,1)}), bf16[16,96,64]{1,2,0:T(8,128)(2,1)S(1)}, u32[]{:S(2)}, u32[]{:S(2)}) async-start(bf16[16,96,64]{1,2,0:T(8,128)(2,1)} %broadcast_in_dim.2), calls=%async_computation | async-start | bytes 524288 | tf_op jit(solution)/shard_map/all_to_all | solution.py:12
  9.6 1.6 %collective-permute-start = (bf16[96,64]{0,1:T(8,128)(2,1)}, bf16[96,64]{0,1:T(8,128)(2,1)S(1)}, u32[]{:S(2)}, u32[]{:S(2)}) collective-permute-start(bf16[96,64]{0,1:T(8,128)(2,1)} %param.5), channel_id=1, source_target_pairs={{0,1},{1,0},{2,3},{3,2},{4,5},{5,4},{6,7},{7,6},{8,9},{9,8},{10,11... | collective-permute-start | bytes 36872 | tf_op jit(solution)/shard_map/ppermute | solution.py:23
  11.2 2.4 %collective-permute-done = bf16[96,64]{0,1:T(8,128)(2,1)S(1)} collective-permute-done((bf16[96,64]{0,1:T(8,128)(2,1)}, bf16[96,64]{0,1:T(8,128)(2,1)S(1)}, u32[]{:S(2)}, u32[]{:S(2)}) %collective-permute-start) | collective-permute-done | bytes 12320 | tf_op jit(solution)/shard_map/ppermute | solution.py:23
  13.6 0.0 copy-done
  13.6 1.1 %fusion.6 = f32[192,64]{0,1:T(8,128)S(1)} fusion(f32[64,64]{1,0:T(8,128)S(1)} %copy-done, bf16[96,64]{0,1:T(8,128)(2,1)S(1)} %collective-permute-done, bf16[96,64]{0,1:T(8,128)(2,1)} %param.5, pred[]{:T(512)S(6)} %eq.3), kind=kOutput, calls=%fused_computation.14 | convolution fusion | flops 9547776 | bytes 90113 | tf_op jit(solution)/shard_map/dot_general | solution.py:29
  14.7 5.0 %all-to-all-done = bf16[16,96,64]{1,2,0:T(8,128)(2,1)S(1)} async-done(((bf16[16,96,64]{1,2,0:T(8,128)(2,1)}), bf16[16,96,64]{1,2,0:T(8,128)(2,1)S(1)}, u32[]{:S(2)}, u32[]{:S(2)}) %all-to-all-start) | async-done | bytes 196640 | tf_op jit(solution)/shard_map/all_to_all | solution.py:12
  19.6 0.2 copy.11
  19.8 0.3 reshape.13
  20.1 0.0 copy-done.2
  20.1 0.0 copy-start.1
  20.1 0.7 %fusion.1 = bf16[192,1536]{1,0:T(8,128)(2,1)S(1)} fusion(f32[192,64]{0,1:T(8,128)S(1)} %fusion.6, bf16[1536,64]{0,1:T(8,128)(2,1)S(1)} %reshape.13, s32[192,1536]{1,0:T(8,128)S(1)} %copy-done.2), kind=kOutput, calls=%fused_computation.2 | convolution fusion | flops 227672064 | bytes 2015232 | tf_op jit(solution)/shard_map/dot_general | solution.py:31
  20.9 0.3 fusion.10
  21.2 0.1 constant_dynamic-slice_fusion
  21.2 0.0 copy-done.1
  21.2 0.3 fusion.5
  21.5 0.1 pad_maximum_fusion
  21.6 1.6 %collective-permute-start.1 = (f32[160,64]{0,1:T(8,128)S(1)}, f32[160,64]{0,1:T(8,128)S(1)}, u32[]{:S(2)}, u32[]{:S(2)}) collective-permute-start(f32[160,64]{0,1:T(8,128)S(1)} %pad_maximum_fusion), channel_id=1, source_target_pairs={{0,1},{1,0},{2,3},{3,2},{4,5},{5,4},{6,7},{7,6},{8,9},{9,8},{10,11... | collective-permute-start | bytes 122888 | tf_op jit(solution)/shard_map/ppermute | solution.py:39
  23.2 0.2 fusion.2
  23.4 0.2 reshape.14
  23.6 1.0 %copy.12 = f32[16,96,64]{1,2,0:T(8,128)} copy(f32[16,96,64]{1,0,2:T(8,128)S(1)} %reshape.14) | data formatting | bytes 786432 | tf_op jit(solution)/shard_map/reshape | solution.py:48
  24.5 3.6 %all-to-all-start.1 = ((f32[16,96,64]{1,2,0:T(8,128)}), f32[16,96,64]{1,2,0:T(8,128)S(1)}, u32[]{:S(2)}, u32[]{:S(2)}) async-start(f32[16,96,64]{1,2,0:T(8,128)} %copy.12), calls=%async_computation.1 | async-start | bytes 1048576 | tf_op jit(solution)/shard_map/all_to_all | solution.py:48
  28.1 0.0 collective-permute-done.1
  28.1 0.1 slice_add_fusion
  28.2 0.3 collective-permute-start.2
  28.5 0.9 %collective-permute-done.2 = f32[64,64]{0,1:T(8,128)S(1)} collective-permute-done((f32[64,64]{0,1:T(8,128)S(1)}, f32[64,64]{0,1:T(8,128)S(1)}, u32[]{:S(2)}, u32[]{:S(2)}) %collective-permute-start.2) | collective-permute-done | bytes 16416 | tf_op jit(solution)/shard_map/ppermute | solution.py:53
  29.4 1.8 %collective-permute-start.3 = (f32[64,64]{0,1:T(8,128)S(1)}, f32[64,64]{0,1:T(8,128)S(1)}, u32[]{:S(2)}, u32[]{:S(2)}) collective-permute-start(f32[64,64]{0,1:T(8,128)S(1)} %add.28), channel_id=1, source_target_pairs={{0,4},{2,6},{4,0},{6,2},{8,12},{10,14},{12,8},{14,10},{16,20},{18,... | collective-permute-start | bytes 49160 | tf_op jit(solution)/shard_map/ppermute | solution.py:53
  31.2 3.5 %collective-permute-done.3 = f32[64,64]{0,1:T(8,128)S(1)} collective-permute-done((f32[64,64]{0,1:T(8,128)S(1)}, f32[64,64]{0,1:T(8,128)S(1)}, u32[]{:S(2)}, u32[]{:S(2)}) %collective-permute-start.3) | collective-permute-done | bytes 16416 | tf_op jit(solution)/shard_map/ppermute | solution.py:53
  34.7 0.8 %collective-permute-start.4 = (f32[64,64]{0,1:T(8,128)S(1)}, f32[64,64]{0,1:T(8,128)S(1)}, u32[]{:S(2)}, u32[]{:S(2)}) collective-permute-start(f32[64,64]{0,1:T(8,128)S(1)} %add.29), channel_id=1, source_target_pairs={{0,8},{2,10},{4,12},{6,14},{8,0},{10,2},{12,4},{14,6},{16,24},{18,... | collective-permute-start | bytes 49160 | tf_op jit(solution)/shard_map/ppermute | solution.py:53
  35.5 3.5 %collective-permute-done.4 = f32[64,64]{0,1:T(8,128)S(1)} collective-permute-done((f32[64,64]{0,1:T(8,128)S(1)}, f32[64,64]{0,1:T(8,128)S(1)}, u32[]{:S(2)}, u32[]{:S(2)}) %collective-permute-start.4) | collective-permute-done | bytes 16416 | tf_op jit(solution)/shard_map/ppermute | solution.py:53
  39.0 3.8 %collective-permute-start.5 = (f32[64,64]{0,1:T(8,128)S(1)}, f32[64,64]{0,1:T(8,128)S(1)}, u32[]{:S(2)}, u32[]{:S(2)}) collective-permute-start(f32[64,64]{0,1:T(8,128)S(1)} %add.30), channel_id=1, source_target_pairs={{0,16},{2,18},{4,20},{6,22},{8,24},{10,26},{12,28},{14,30},{16,0},... | collective-permute-start | bytes 49160 | tf_op jit(solution)/shard_map/ppermute | solution.py:53
  42.8 0.9 %convolution_multiply_fusion = f32[96,64]{0,1:T(8,128)} fusion(f32[64,64]{1,0:T(8,128)S(1)} %copy-done, f32[160,64]{0,1:T(8,128)S(1)} %collective-permute-done.1, f32[192,64]{0,1:T(8,128)S(1)} %fusion.10, s32[]{:T(128)S(6)} %select_n.16), kind=kOutput, calls=%fused_computation.3 | convolution fusion | flops 4730880 | bytes 122884 | tf_op jit(solution)/shard_map/dot_general | solution.py:55
  43.7 1.0 %collective-permute-done.5 = f32[64,64]{0,1:T(8,128)S(1)} collective-permute-done((f32[64,64]{0,1:T(8,128)S(1)}, f32[64,64]{0,1:T(8,128)S(1)}, u32[]{:S(2)}, u32[]{:S(2)}) %collective-permute-start.5) | collective-permute-done | bytes 16416 | tf_op jit(solution)/shard_map/ppermute | solution.py:53
  44.7 0.7 %copy.13 = f32[64,64]{1,0:T(8,128)} copy(f32[64,64]{0,1:T(8,128)S(1)} %add_multiply_fusion) | data formatting | bytes 32768
  45.4 0.0 all-to-all-done.1
  45.5 0.6 %broadcast_multiply_fusion = f32[96,64]{0,1:T(8,128)} fusion(f32[96,64]{0,1:T(8,128)S(1)} %reduce_sum.9), kind=kLoop, calls=%fused_computation.12 | loop fusion | flops 6144 | bytes 49152 | tf_op jit(solution)/shard_map/mul | solution.py:56
  (5 shorter events, 0.1 us)
Async XLA Ops:
  0.6 13.0 %copy-start = (f32[64,64]{1,0:T(8,128)S(1)}, f32[64,64]{1,0:T(8,128)}, u32[]{:S(2)}) copy-start(f32[64,64]{1,0:T(8,128)} %param.7) | copy-start | bytes 49156
  0.6 19.4 %copy-start.2 = (s32[192,1536]{1,0:T(8,128)S(1)}, s32[192,1536]{1,0:T(8,128)}, u32[]{:S(2)}) copy-start(s32[192,1536]{1,0:T(8,128)} %param.4) | copy-start | bytes 3538948
  2.2 17.4 %all-to-all-start = ((bf16[16,96,64]{1,2,0:T(8,128)(2,1)}), bf16[16,96,64]{1,2,0:T(8,128)(2,1)S(1)}, u32[]{:S(2)}, u32[]{:S(2)}) async-start(bf16[16,96,64]{1,2,0:T(8,128)(2,1)} %broadcast_in_dim.2), calls=%async_computation | async-start | bytes 524288 | tf_op jit(solution)/shard_map/all_to_all | solution.py:12
  9.6 4.0 %collective-permute-start = (bf16[96,64]{0,1:T(8,128)(2,1)}, bf16[96,64]{0,1:T(8,128)(2,1)S(1)}, u32[]{:S(2)}, u32[]{:S(2)}) collective-permute-start(bf16[96,64]{0,1:T(8,128)(2,1)} %param.5), channel_id=1, source_target_pairs={{0,1},{1,0},{2,3},{3,2},{4,5},{5,4},{6,7},{7,6},{8,9},{9,8},{10,11... | collective-permute-start | bytes 36872 | tf_op jit(solution)/shard_map/ppermute | solution.py:23
  20.1 1.2 %copy-start.1 = (bf16[96,64]{0,1:T(8,128)(2,1)S(1)}, bf16[96,64]{0,1:T(8,128)(2,1)}, u32[]{:S(2)}) copy-start(bf16[96,64]{0,1:T(8,128)(2,1)} %param.5) | copy-start | bytes 36868
  21.6 6.5 %collective-permute-start.1 = (f32[160,64]{0,1:T(8,128)S(1)}, f32[160,64]{0,1:T(8,128)S(1)}, u32[]{:S(2)}, u32[]{:S(2)}) collective-permute-start(f32[160,64]{0,1:T(8,128)S(1)} %pad_maximum_fusion), channel_id=1, source_target_pairs={{0,1},{1,0},{2,3},{3,2},{4,5},{5,4},{6,7},{7,6},{8,9},{9,8},{10,11... | collective-permute-start | bytes 122888 | tf_op jit(solution)/shard_map/ppermute | solution.py:39
  24.5 20.9 %all-to-all-start.1 = ((f32[16,96,64]{1,2,0:T(8,128)}), f32[16,96,64]{1,2,0:T(8,128)S(1)}, u32[]{:S(2)}, u32[]{:S(2)}) async-start(f32[16,96,64]{1,2,0:T(8,128)} %copy.12), calls=%async_computation.1 | async-start | bytes 1048576 | tf_op jit(solution)/shard_map/all_to_all | solution.py:48
  28.2 1.2 %collective-permute-start.2 = (f32[64,64]{0,1:T(8,128)S(1)}, f32[64,64]{0,1:T(8,128)S(1)}, u32[]{:S(2)}, u32[]{:S(2)}) collective-permute-start(f32[64,64]{0,1:T(8,128)S(1)} %slice_add_fusion), channel_id=1, source_target_pairs={{0,2},{2,0},{4,6},{6,4},{8,10},{10,8},{12,14},{14,12},{16,18},{18,... | collective-permute-start | bytes 49160 | tf_op jit(solution)/shard_map/ppermute | solution.py:53
  29.4 5.3 %collective-permute-start.3 = (f32[64,64]{0,1:T(8,128)S(1)}, f32[64,64]{0,1:T(8,128)S(1)}, u32[]{:S(2)}, u32[]{:S(2)}) collective-permute-start(f32[64,64]{0,1:T(8,128)S(1)} %add.28), channel_id=1, source_target_pairs={{0,4},{2,6},{4,0},{6,2},{8,12},{10,14},{12,8},{14,10},{16,20},{18,... | collective-permute-start | bytes 49160 | tf_op jit(solution)/shard_map/ppermute | solution.py:53
  34.7 4.3 %collective-permute-start.4 = (f32[64,64]{0,1:T(8,128)S(1)}, f32[64,64]{0,1:T(8,128)S(1)}, u32[]{:S(2)}, u32[]{:S(2)}) collective-permute-start(f32[64,64]{0,1:T(8,128)S(1)} %add.29), channel_id=1, source_target_pairs={{0,8},{2,10},{4,12},{6,14},{8,0},{10,2},{12,4},{14,6},{16,24},{18,... | collective-permute-start | bytes 49160 | tf_op jit(solution)/shard_map/ppermute | solution.py:53
  39.0 5.7 %collective-permute-start.5 = (f32[64,64]{0,1:T(8,128)S(1)}, f32[64,64]{0,1:T(8,128)S(1)}, u32[]{:S(2)}, u32[]{:S(2)}) collective-permute-start(f32[64,64]{0,1:T(8,128)S(1)} %add.30), channel_id=1, source_target_pairs={{0,16},{2,18},{4,20},{6,22},{8,24},{10,26},{12,28},{14,30},{16,0},... | collective-permute-start | bytes 49160 | tf_op jit(solution)/shard_map/ppermute | solution.py:53

commit v3 on v1

v3 whole, which is shorter than its diff:
```python
import jax
import jax.numpy as jnp
from jax import lax
from jax.sharding import Mesh, PartitionSpec as P

HI = lax.Precision.HIGHEST
SWAP = [(0, 1), (1, 0)]
ROW = ("chip", "core")
TREE_GATHER = False


def gather_rows(x, axis):
    n = lax.axis_size(axis)
    slots = jnp.broadcast_to(x[None], (n,) + x.shape)
    got = lax.all_to_all(slots, axis, 0, 0)
    return got.reshape((n * x.shape[0],) + x.shape[1:])


def tree_gather(x, axis):
    n = lax.axis_size(axis)
    me = lax.axis_index(axis)
    bits = []
    b = n // 2
    while b >= 1:
        bits.append(b)
        b //= 2
    held = x[None]
    for b in bits:
        held = jnp.concatenate([held, lax.ppermute(held, axis, [(i, i ^ b) for i in range(n)])])
    rel = me ^ jnp.arange(n)
    slot = sum(((rel // b) % 2) << j for j, b in enumerate(bits))
    return jnp.take(held, slot, axis=0).reshape((n * x.shape[0],) + x.shape[1:])


def shards(counts, theta, phi, affinity):
    nr, nc = lax.axis_size(ROW), lax.axis_size("col")
    assert nr & (nr - 1) == 0
    nodes = theta.shape[0] * nr * nc
    inverse = 1.0 / nodes
    k = theta.shape[1]
    c = lax.axis_index("col")
    r = lax.axis_index(ROW)
    if nc == 2:
        other = lax.ppermute(theta, "col", SWAP)
        theta_rows = jnp.where(c == 0, jnp.concatenate([theta, other]), jnp.concatenate([other, theta]))
    else:
        theta_rows = gather_rows(theta, "col")
    nchip = lax.axis_size("chip")
    core = lax.axis_index("core")
    by_chip = lax.all_to_all(jnp.broadcast_to(phi[None], (nchip,) + phi.shape), "chip", 0, 0)
    other = lax.ppermute(by_chip, "core", SWAP)
    pair = jnp.where(core == 0, jnp.stack([by_chip, other], axis=1), jnp.stack([other, by_chip], axis=1))
    members = pair.reshape(nr * phi.shape[0], k)
    theta_wide = theta_rows.astype(jnp.float32)
    row_factor = jnp.dot(theta_wide, affinity, precision=HI)
    factor_half = row_factor.astype(jnp.bfloat16)
    rate = jnp.dot(row_factor, members.astype(jnp.float32).T, precision=HI)
    ratio = (1.0 - counts.astype(jnp.float32) / rate).astype(jnp.bfloat16)
    gphi = jnp.dot(ratio, members, preferred_element_type=jnp.float32)
    gcol = lax.dot_general(ratio, factor_half, (((0,), (0,)), ((), ())), preferred_element_type=jnp.float32)
    part = jnp.dot(theta_wide.T, gphi, precision=HI)
    mc = gphi.shape[0] // nc
    if nc == 2:
        send = jnp.concatenate([lax.dynamic_slice_in_dim(gphi, (1 - c) * mc, mc), part])
        got = lax.ppermute(send, "col", SWAP)
        gphi_sum = lax.dynamic_slice_in_dim(gphi, c * mc, mc) + got[:mc]
        part_sum = part + got[mc:]
    else:
        slots = jnp.concatenate([gphi.reshape(nc, mc, k), jnp.broadcast_to(part[None], (nc, k, k))], axis=1)
        got = lax.all_to_all(slots, "col", 0, 0)
        gphi_sum = jnp.sum(got[:, :mc], axis=0)
        part_sum = jnp.sum(got[:, mc:], axis=0)
    mr = gcol.shape[0] // nr
    acc = gcol.reshape(nr, mr, k)
    b = 1
    while b < nr:
        pairs = acc.reshape(acc.shape[0] // 2, 2, mr, k)
        mine = (r // b) % 2
        keep = jnp.take(pairs, mine, axis=1)
        away = jnp.take(pairs, 1 - mine, axis=1)
        send = jnp.concatenate([away.reshape(-1, k), part_sum])
        got = lax.ppermute(send, ROW, [(i, i ^ b) for i in range(nr)])
        acc = keep + got[: keep.shape[0] * mr].reshape(keep.shape)
        part_sum = part_sum + got[keep.shape[0] * mr:]
        b *= 2
    phi_sum = acc[0]
    theta_grad = inverse * jnp.dot(gphi_sum, affinity.T, precision=HI)
    phi_grad = inverse * phi_sum
    affinity_grad = inverse * inverse * part_sum
    return (theta_grad, phi_grad, affinity_grad)


def solution(mesh):
    rows, cols = mesh.devices.shape
    split = Mesh(mesh.devices.reshape(rows // 2, 2, cols), ("chip", "core", "col"))
    placed = (P(ROW, "col"), P(ROW + ("col",), None), P(("col",) + ROW, None), P())
    return jax.shard_map(
        shards,
        mesh=split,
        in_specs=placed,
        out_specs=(P(ROW + ("col",), None), P(("col",) + ROW, None), P()),
        check_vma=False,
    )
```

time: 57.2 us -> 45.1 us (0.79)
  the two profiles are of different devices: /device:TPU:11 before, /device:TPU:0 now
where the time goes in v3:
time: 45.1 us; the launch traced here: 44.5 us
  waiting for transfers between devices  22.6 us (50%)
  starting transfers between devices  11.2 us (25%)
  local copies, waits for them, and re-layouts  4.89 us (11%)
  matrix products  3.41 us (8%)
  other arithmetic  1.45 us (3%)
  between operations  1.02 us (2%)
    ppermute x4, waiting for transfers between devices, shards(): got = lax.ppermute(send, ROW, [(i, i ^ b) for i in range(nr)])  15 us
    all_to_all x1, starting transfers between devices, shards(): lax.all_to_all(jnp.broadcast_to(phi[None], (nchip,) + phi.shape), 'chip',...  7.25 us
    all_to_all x1, waiting for transfers between devices, shards(): lax.all_to_all(jnp.broadcast_to(phi[None], (nchip,) + phi.shape), 'chip',...  5.82 us
    ppermute x1, starting transfers between devices, shards(): got = lax.ppermute(send, 'col', SWAP)  1.58 us
    ppermute x1, starting transfers between devices, shards(): other = lax.ppermute(theta, 'col', SWAP)  1.52 us
    broadcast_in_dim x1, local copies, waits for them, and re-layouts, shards(): jnp.broadcast_to(phi[None], (nchip,) + phi.shape)  1.48 us
    ppermute x1, waiting for transfers between devices, shards(): got = lax.ppermute(send, 'col', SWAP)  1.46 us
    dot_general x1, matrix products, shards(): row_factor = jnp.dot(theta_wide, affinity, precision=HI)  1.06 us
  transfers between devices with their start and end apart: 8, of which 7 were waited for; matrix products, arithmetic and copies ran while one was open for 7% of the time, Pallas kernels for 0%

profile of v3, /device:TPU:0, one launch (start us, length us, event | category | flops | bytes accessed | tf_op | source)
XLA Modules:
  0.0 44.5 jit_solution(8302520090491117679)
XLA Ops:
  0.6 0.0 copy-start
  0.6 0.0 copy-start.2
  0.7 1.5 %broadcast_in_dim.42 = bf16[8,96,64]{1,2,0:T(8,128)(2,1)} broadcast(bf16[96,64]{0,1:T(8,128)(2,1)} %param.14), dimensions={1,2} | broadcast | bytes 110592 | tf_op jit(solution)/shard_map/broadcast_in_dim | solution.py:50
  2.1 7.3 %all-to-all-start = ((bf16[8,96,64]{1,2,0:T(8,128)(2,1)}), bf16[8,96,64]{1,2,0:T(8,128)(2,1)S(1)}, u32[]{:S(2)}, u32[]{:S(2)}) async-start(bf16[8,96,64]{1,2,0:T(8,128)(2,1)} %broadcast_in_dim.42), calls=%async_computation | async-start | bytes 262144 | tf_op jit(solution)/shard_map/all_to_all | solution.py:50
  9.4 1.5 %collective-permute-start = (bf16[96,64]{0,1:T(8,128)(2,1)}, bf16[96,64]{0,1:T(8,128)(2,1)S(1)}, u32[]{:S(2)}, u32[]{:S(2)}) collective-permute-start(bf16[96,64]{0,1:T(8,128)(2,1)} %param.13), channel_id=1, source_target_pairs={{0,1},{1,0},{2,3},{3,2},{4,5},{5,4},{6,7},{7,6},{8,9},{9,8},{10,11... | collective-permute-start | bytes 36872 | tf_op jit(solution)/shard_map/ppermute | solution.py:44
  10.9 5.8 %all-to-all-done = bf16[8,96,64]{1,2,0:T(8,128)(2,1)S(1)} async-done(((bf16[8,96,64]{1,2,0:T(8,128)(2,1)}), bf16[8,96,64]{1,2,0:T(8,128)(2,1)S(1)}, u32[]{:S(2)}, u32[]{:S(2)}) %all-to-all-start) | async-done | bytes 98336 | tf_op jit(solution)/shard_map/all_to_all | solution.py:50
  16.7 0.0 collective-permute-start.1
  16.7 0.0 collective-permute-done
  16.7 0.0 copy-done
  16.7 1.1 %fusion.15 = f32[192,64]{0,1:T(8,128)S(1)} fusion(f32[64,64]{1,0:T(8,128)S(1)} %copy-done, bf16[96,64]{0,1:T(8,128)(2,1)S(1)} %collective-permute-done, bf16[96,64]{0,1:T(8,128)(2,1)} %param.13, pred[]{:T(512)S(6)} %eq.11), kind=kOutput, calls=%fused_computation.38 | convolution fusion | flops 9547776 | bytes 90113 | tf_op jit(solution)/shard_map/dot_general | solution.py:55
  17.8 0.3 collective-permute-done.1
  18.1 0.1 maximum_select_fusion
  18.2 0.3 copy.30
  18.5 0.3 select_n.92
  18.7 0.0 copy-done.2
  18.7 0.7 %fusion.1 = bf16[192,1536]{1,0:T(8,128)(2,1)S(1)} fusion(f32[192,64]{0,1:T(8,128)S(1)} %fusion.15, bf16[1536,64]{0,1:T(8,128)(2,1)S(1)} %select_n.92, s32[192,1536]{1,0:T(8,128)S(1)} %copy-done.2), kind=kOutput, calls=%fused_computation.2 | convolution fusion | flops 227672064 | bytes 2015232 | tf_op jit(solution)/shard_map/dot_general | solution.py:57
  19.5 0.0 copy-start.1
  19.5 0.3 fusion.19
  19.8 0.2 fusion.11
  20.0 0.1 constant_dynamic-slice_fusion.2
  20.1 0.1 copy-done.1
  20.2 0.2 fusion.14
  20.4 0.1 pad_maximum_fusion.2
  20.5 1.6 %collective-permute-start.2 = (f32[160,64]{0,1:T(8,128)S(1)}, f32[160,64]{0,1:T(8,128)S(1)}, u32[]{:S(2)}, u32[]{:S(2)}) collective-permute-start(f32[160,64]{0,1:T(8,128)S(1)} %pad_maximum_fusion.2), channel_id=1, source_target_pairs={{0,1},{1,0},{2,3},{3,2},{4,5},{5,4},{6,7},{7,6},{8,9},{9,8},{10,11... | collective-permute-start | bytes 122888 | tf_op jit(solution)/shard_map/ppermute | solution.py:65
  22.1 0.7 %reshape_reshape.3 = f32[8,2,96,64]{2,1,0,3:T(2,128)S(1)} reshape(f32[1536,64]{0,1:T(8,128)S(1)} %fusion.11) | data formatting | bytes 786432 | tf_op jit(solution)/shard_map/reshape;reshape | solution.py:77
  22.8 0.5 %constant_dynamic-slice_fusion.1 = (f32[8,1,96,64]{2,1,0,3:T(1,128)S(1)}, f32[8,1,96,64]{2,1,0,3:T(1,128)S(1)}) fusion(f32[8,2,96,64]{2,1,0,3:T(2,128)S(1)} %reshape_reshape.3, s32[]{:T(128)S(6)} %select_n.124, s32[]{:T(128)S(6)} %select_n.126), kind=kLoop, calls=%fused_computation.40 | loop fusion | bytes 786440 | tf_op jit(solution)/shard_map/jit(_take) | solution.py:79
  23.3 0.1 reshape.59
  23.4 1.5 %collective-permute-done.2 = f32[160,64]{0,1:T(8,128)S(1)} collective-permute-done((f32[160,64]{0,1:T(8,128)S(1)}, f32[160,64]{0,1:T(8,128)S(1)}, u32[]{:S(2)}, u32[]{:S(2)}) %collective-permute-start.2) | collective-permute-done | bytes 40992 | tf_op jit(solution)/shard_map/ppermute | solution.py:65
  24.9 0.1 slice_add_fusion.4
  25.0 0.1 collective-permute-start.3
  25.1 1.4 %collective-permute-done.3 = f32[832,64]{0,1:T(8,128)S(1)} collective-permute-done((f32[832,64]{0,1:T(8,128)S(1)}, f32[832,64]{0,1:T(8,128)S(1)}, u32[]{:S(2)}, u32[]{:S(2)}) %collective-permute-start.3) | collective-permute-done | bytes 213024 | tf_op jit(solution)/shard_map/ppermute | solution.py:82
  26.5 0.1 reshape.60
  26.7 0.1 fusion.3
  26.8 0.1 copy.34
  26.9 0.1 reshape.62
  27.1 0.3 collective-permute-start.4
  27.4 5.3 %collective-permute-done.4 = f32[448,64]{0,1:T(8,128)S(1)} collective-permute-done((f32[448,64]{0,1:T(8,128)S(1)}, f32[448,64]{0,1:T(8,128)S(1)}, u32[]{:S(2)}, u32[]{:S(2)}) %collective-permute-start.4) | collective-permute-done | bytes 114720 | tf_op jit(solution)/shard_map/ppermute | solution.py:82
  32.7 0.1 reshape.63
  32.9 0.1 copy.37
  32.9 0.1 reshape.65
  33.1 0.1 pad_maximum_fusion.3
  33.1 0.0 collective-permute-start.5
  33.2 4.2 %collective-permute-done.5 = f32[256,64]{0,1:T(8,128)S(1)} collective-permute-done((f32[256,64]{0,1:T(8,128)S(1)}, f32[256,64]{0,1:T(8,128)S(1)}, u32[]{:S(2)}, u32[]{:S(2)}) %collective-permute-start.5) | collective-permute-done | bytes 65568 | tf_op jit(solution)/shard_map/ppermute | solution.py:82
  37.4 0.1 reshape.66
  37.6 0.1 slice_add_fusion.1
  37.6 0.1 pad_maximum_fusion.4
  37.7 0.5 %collective-permute-start.6 = (f32[160,64]{0,1:T(8,128)S(1)}, f32[160,64]{0,1:T(8,128)S(1)}, u32[]{:S(2)}, u32[]{:S(2)}) collective-permute-start(f32[160,64]{0,1:T(8,128)S(1)} %pad_maximum_fusion.4), channel_id=1, source_target_pairs={{0,16},{2,18},{4,20},{6,22},{8,24},{10,26},{12,28},{14,30},{16,0},... | collective-permute-start | bytes 122888 | tf_op jit(solution)/shard_map/ppermute | solution.py:82
  38.2 0.9 %convolution_multiply_fusion = f32[96,64]{0,1:T(8,128)} fusion(f32[64,64]{1,0:T(8,128)S(1)} %copy-done, f32[160,64]{0,1:T(8,128)S(1)} %collective-permute-done.2, f32[192,64]{0,1:T(8,128)S(1)} %fusion.19, s32[]{:T(128)S(6)} %select_n.93), kind=kOutput, calls=%fused_computation.3 | convolution fusion | flops 4730880 | bytes 122884 | tf_op jit(solution)/shard_map/dot_general | solution.py:87
  39.0 4.1 %collective-permute-done.6 = f32[160,64]{0,1:T(8,128)S(1)} collective-permute-done((f32[160,64]{0,1:T(8,128)S(1)}, f32[160,64]{0,1:T(8,128)S(1)}, u32[]{:S(2)}, u32[]{:S(2)}) %collective-permute-start.6) | collective-permute-done | bytes 40992 | tf_op jit(solution)/shard_map/ppermute | solution.py:82
  43.1 0.1 fusion.7
  43.2 0.7 %copy.39 = f32[64,64]{1,0:T(8,128)} copy(f32[64,64]{0,1:T(8,128)S(1)} %fusion.7) | data formatting | bytes 32768
  43.9 0.6 %fusion.10 = f32[96,64]{0,1:T(8,128)} fusion(f32[160,64]{0,1:T(8,128)S(1)} %collective-permute-done.6, f32[1,2,96,64]{2,3,1,0:T(8,128)S(1)} %fusion.6, s32[]{:T(128)S(6)} %select_n.136, pred[]{:T(512)S(6)} %and.72), kind=kLoop, calls=%fused_computation.26 | loop fusion | flops 18432 | bytes 73733 | tf_op jit(solution)/shard_map/mul | solution.py:88
  (12 shorter events, 0.2 us)
Async XLA Ops:
  0.6 16.1 %copy-start = (f32[64,64]{1,0:T(8,128)S(1)}, f32[64,64]{1,0:T(8,128)}, u32[]{:S(2)}) copy-start(f32[64,64]{1,0:T(8,128)} %param.15) | copy-start | bytes 49156
  0.6 18.1 %copy-start.2 = (s32[192,1536]{1,0:T(8,128)S(1)}, s32[192,1536]{1,0:T(8,128)}, u32[]{:S(2)}) copy-start(s32[192,1536]{1,0:T(8,128)} %param.12) | copy-start | bytes 3538948
  2.1 14.6 %all-to-all-start = ((bf16[8,96,64]{1,2,0:T(8,128)(2,1)}), bf16[8,96,64]{1,2,0:T(8,128)(2,1)S(1)}, u32[]{:S(2)}, u32[]{:S(2)}) async-start(bf16[8,96,64]{1,2,0:T(8,128)(2,1)} %broadcast_in_dim.42), calls=%async_computation | async-start | bytes 262144 | tf_op jit(solution)/shard_map/all_to_all | solution.py:50
  9.4 7.3 %collective-permute-start = (bf16[96,64]{0,1:T(8,128)(2,1)}, bf16[96,64]{0,1:T(8,128)(2,1)S(1)}, u32[]{:S(2)}, u32[]{:S(2)}) collective-permute-start(bf16[96,64]{0,1:T(8,128)(2,1)} %param.13), channel_id=1, source_target_pairs={{0,1},{1,0},{2,3},{3,2},{4,5},{5,4},{6,7},{7,6},{8,9},{9,8},{10,11... | collective-permute-start | bytes 36872 | tf_op jit(solution)/shard_map/ppermute | solution.py:44
  16.7 1.3 %collective-permute-start.1 = (bf16[8,96,64]{1,2,0:T(8,128)(2,1)S(1)}, bf16[8,96,64]{1,2,0:T(8,128)(2,1)S(1)}, u32[]{:S(2)}, u32[]{:S(2)}) collective-permute-start(bf16[8,96,64]{1,2,0:T(8,128)(2,1)S(1)} %all-to-all-done), channel_id=1, source_target_pairs={{0,2},{2,0},{1,3},{3,1},{4,6},{6,4},{5,7},{7,5},{8,10},{10,8},{9,1... | collective-permute-start | bytes 294920 | tf_op jit(solution)/shard_map/ppermute | solution.py:51
  19.5 0.7 %copy-start.1 = (bf16[96,64]{0,1:T(8,128)(2,1)S(1)}, bf16[96,64]{0,1:T(8,128)(2,1)}, u32[]{:S(2)}) copy-start(bf16[96,64]{0,1:T(8,128)(2,1)} %param.13) | copy-start | bytes 36868
  20.5 4.3 %collective-permute-start.2 = (f32[160,64]{0,1:T(8,128)S(1)}, f32[160,64]{0,1:T(8,128)S(1)}, u32[]{:S(2)}, u32[]{:S(2)}) collective-permute-start(f32[160,64]{0,1:T(8,128)S(1)} %pad_maximum_fusion.2), channel_id=1, source_target_pairs={{0,1},{1,0},{2,3},{3,2},{4,5},{5,4},{6,7},{7,6},{8,9},{9,8},{10,11... | collective-permute-start | bytes 122888 | tf_op jit(solution)/shard_map/ppermute | solution.py:65
  25.0 1.6 %collective-permute-start.3 = (f32[832,64]{0,1:T(8,128)S(1)}, f32[832,64]{0,1:T(8,128)S(1)}, u32[]{:S(2)}, u32[]{:S(2)}) collective-permute-start(f32[832,64]{0,1:T(8,128)S(1)} %pad_maximum_fusion), channel_id=1, source_target_pairs={{0,2},{2,0},{4,6},{6,4},{8,10},{10,8},{12,14},{14,12},{16,18},{18,... | collective-permute-start | bytes 638984 | tf_op jit(solution)/shard_map/ppermute | solution.py:82
  27.1 5.6 %collective-permute-start.4 = (f32[448,64]{0,1:T(8,128)S(1)}, f32[448,64]{0,1:T(8,128)S(1)}, u32[]{:S(2)}, u32[]{:S(2)}) collective-permute-start(f32[448,64]{0,1:T(8,128)S(1)} %pad_maximum_fusion.1), channel_id=1, source_target_pairs={{0,4},{2,6},{4,0},{6,2},{8,12},{10,14},{12,8},{14,10},{16,20},{18,... | collective-permute-start | bytes 344072 | tf_op jit(solution)/shard_map/ppermute | solution.py:82
  33.1 4.3 %collective-permute-start.5 = (f32[256,64]{0,1:T(8,128)S(1)}, f32[256,64]{0,1:T(8,128)S(1)}, u32[]{:S(2)}, u32[]{:S(2)}) collective-permute-start(f32[256,64]{0,1:T(8,128)S(1)} %pad_maximum_fusion.3), channel_id=1, source_target_pairs={{0,8},{2,10},{4,12},{6,14},{8,0},{10,2},{12,4},{14,6},{16,24},{18,... | collective-permute-start | bytes 196616 | tf_op jit(solution)/shard_map/ppermute | solution.py:82
  37.7 5.4 %collective-permute-start.6 = (f32[160,64]{0,1:T(8,128)S(1)}, f32[160,64]{0,1:T(8,128)S(1)}, u32[]{:S(2)}, u32[]{:S(2)}) collective-permute-start(f32[160,64]{0,1:T(8,128)S(1)} %pad_maximum_fusion.4), channel_id=1, source_target_pairs={{0,16},{2,18},{4,20},{6,22},{8,24},{10,26},{12,28},{14,30},{16,0},... | collective-permute-start | bytes 122888 | tf_op jit(solution)/shard_map/ppermute | solution.py:82

commit v4 on v3

--- a/solution.py
+++ b/solution.py
@@ -73,7 +73,7 @@
     mr = gcol.shape[0] // nr
     acc = gcol.reshape(nr, mr, k)
     b = 1
-    while b < nr:
+    while b < nr // 4:
         pairs = acc.reshape(acc.shape[0] // 2, 2, mr, k)
         mine = (r // b) % 2
         keep = jnp.take(pairs, mine, axis=1)
@@ -83,6 +83,23 @@
         acc = keep + got[: keep.shape[0] * mr].reshape(keep.shape)
         part_sum = part_sum + got[keep.shape[0] * mr:]
         b *= 2
+    if acc.shape[0] == 4:
+        quad = (r // b) % 4
+        held = [part_sum]
+        total = jnp.take(acc, quad, axis=0)
+        for s in (1, 2, 3):
+            send = jnp.concatenate([jnp.take(acc, quad ^ s, axis=0), part_sum])
+            got = lax.ppermute(send, ROW, [(i, i ^ (s * b)) for i in range(nr)])
+            total = total + got[:mr]
+            held.append(got[mr:])
+        part_sum = jnp.sum(jnp.take(jnp.stack(held), quad ^ jnp.arange(4), axis=0), axis=0)
+        acc = total[None]
+    elif acc.shape[0] == 2:
+        mine = (r // b) % 2
+        send = jnp.concatenate([jnp.take(acc, 1 - mine, axis=0), part_sum])
+        got = lax.ppermute(send, ROW, [(i, i ^ b) for i in range(nr)])
+        acc = (jnp.take(acc, mine, axis=0) + got[:mr])[None]
+        part_sum = part_sum + got[mr:]
     phi_sum = acc[0]
     theta_grad = inverse * jnp.dot(gphi_sum, affinity.T, precision=HI)
     phi_grad = inverse * phi_sum

time: 45.1 us -> 44 us (0.976)
  waiting for transfers between devices: 22.6 us -> 17.1 us
  starting transfers between devices: 11.2 us -> 15.2 us
  local copies, waits for them, and re-layouts: 4.89 us -> 5.41 us
    ppermute x4 -> x2, waiting for transfers between devices: 15 us -> 6.7 us  [shards(): got = lax.ppermute(send, ROW, [(i, i ^ b) for i in range(nr)])]
    ppermute x0 -> x3, starting transfers between devices: none -> 4.45 us  [shards(): got = lax.ppermute(send, ROW, [(i, i ^ s * b) for i in range(nr)])]
    ppermute x0 -> x3, waiting for transfers between devices: none -> 2.8 us  [shards(): got = lax.ppermute(send, ROW, [(i, i ^ s * b) for i in range(nr)])]
    gather x0 -> x1, local copies, waits for them, and re-layouts: none -> 0.56 us  [shards(): jnp.take(jnp.stack(held), quad ^ jnp.arange(4), axis=0)]
    ppermute x4 -> x2, starting transfers between devices: 0.82 us -> 0.35 us  [shards(): got = lax.ppermute(send, ROW, [(i, i ^ b) for i in range(nr)])]
  transfers between devices with their start and end apart: 8 -> 9, of which waited for: 7 -> 8; matrix products, arithmetic and copies ran while one was open for 7% -> 8% of each run, Pallas kernels for 0% -> 0%
where the time goes in v4:
time: 44 us; the launch traced here: 43.3 us
  waiting for transfers between devices  17.1 us (39%)
  starting transfers between devices  15.2 us (35%)
  local copies, waits for them, and re-layouts  5.41 us (12%)
  matrix products  3.41 us (8%)
  other arithmetic  1.32 us (3%)
  between operations  0.99 us (2%)
    all_to_all x1, starting transfers between devices, shards(): lax.all_to_all(jnp.broadcast_to(phi[None], (nchip,) + phi.shape), 'chip',...  7.25 us
    ppermute x2, waiting for transfers between devices, shards(): got = lax.ppermute(send, ROW, [(i, i ^ b) for i in range(nr)])  6.7 us
    all_to_all x1, waiting for transfers between devices, shards(): lax.all_to_all(jnp.broadcast_to(phi[None], (nchip,) + phi.shape), 'chip',...  5.82 us
    ppermute x3, starting transfers between devices, shards(): got = lax.ppermute(send, ROW, [(i, i ^ s * b) for i in range(nr)])  4.45 us
    ppermute x3, waiting for transfers between devices, shards(): got = lax.ppermute(send, ROW, [(i, i ^ s * b) for i in range(nr)])  2.8 us
    ppermute x1, starting transfers between devices, shards(): got = lax.ppermute(send, 'col', SWAP)  1.58 us
    ppermute x1, starting transfers between devices, shards(): other = lax.ppermute(theta, 'col', SWAP)  1.52 us
    broadcast_in_dim x1, local copies, waits for them, and re-layouts, shards(): jnp.broadcast_to(phi[None], (nchip,) + phi.shape)  1.48 us
  transfers between devices with their start and end apart: 9, of which 8 were waited for; matrix products, arithmetic and copies ran while one was open for 8% of the time, Pallas kernels for 0%

profile of v4, /device:TPU:0, one launch (start us, length us, event | category | flops | bytes accessed | tf_op | source)
XLA Modules:
  0.0 43.3 jit_solution(9047396795352885252)
XLA Ops:
  0.6 0.0 copy-start
  0.6 0.0 copy-start.2
  0.7 1.5 %broadcast_in_dim.43 = bf16[8,96,64]{1,2,0:T(8,128)(2,1)} broadcast(bf16[96,64]{0,1:T(8,128)(2,1)} %param.12), dimensions={1,2} | broadcast | bytes 110592 | tf_op jit(solution)/shard_map/broadcast_in_dim | solution.py:50
  2.1 7.3 %all-to-all-start = ((bf16[8,96,64]{1,2,0:T(8,128)(2,1)}), bf16[8,96,64]{1,2,0:T(8,128)(2,1)S(1)}, u32[]{:S(2)}, u32[]{:S(2)}) async-start(bf16[8,96,64]{1,2,0:T(8,128)(2,1)} %broadcast_in_dim.43), calls=%async_computation | async-start | bytes 262144 | tf_op jit(solution)/shard_map/all_to_all | solution.py:50
  9.4 1.5 %collective-permute-start = (bf16[96,64]{0,1:T(8,128)(2,1)}, bf16[96,64]{0,1:T(8,128)(2,1)S(1)}, u32[]{:S(2)}, u32[]{:S(2)}) collective-permute-start(bf16[96,64]{0,1:T(8,128)(2,1)} %param.11), channel_id=1, source_target_pairs={{0,1},{1,0},{2,3},{3,2},{4,5},{5,4},{6,7},{7,6},{8,9},{9,8},{10,11... | collective-permute-start | bytes 36872 | tf_op jit(solution)/shard_map/ppermute | solution.py:44
  10.9 5.8 %all-to-all-done = bf16[8,96,64]{1,2,0:T(8,128)(2,1)S(1)} async-done(((bf16[8,96,64]{1,2,0:T(8,128)(2,1)}), bf16[8,96,64]{1,2,0:T(8,128)(2,1)S(1)}, u32[]{:S(2)}, u32[]{:S(2)}) %all-to-all-start) | async-done | bytes 98336 | tf_op jit(solution)/shard_map/all_to_all | solution.py:50
  16.7 0.0 collective-permute-start.1
  16.7 0.0 collective-permute-done
  16.7 0.0 copy-done
  16.7 1.1 %fusion.11 = f32[192,64]{0,1:T(8,128)S(1)} fusion(f32[64,64]{1,0:T(8,128)S(1)} %copy-done, bf16[96,64]{0,1:T(8,128)(2,1)S(1)} %collective-permute-done, bf16[96,64]{0,1:T(8,128)(2,1)} %param.11, pred[]{:T(512)S(6)} %eq.10), kind=kOutput, calls=%fused_computation.42 | convolution fusion | flops 9547776 | bytes 90113 | tf_op jit(solution)/shard_map/dot_general | solution.py:55
  17.8 0.3 collective-permute-done.1
  18.1 0.1 maximum_select_fusion
  18.2 0.3 copy.24
  18.5 0.3 select_n.91
  18.7 0.0 copy-done.2
  18.7 0.7 %fusion.1 = bf16[192,1536]{1,0:T(8,128)(2,1)S(1)} fusion(f32[192,64]{0,1:T(8,128)S(1)} %fusion.11, bf16[1536,64]{0,1:T(8,128)(2,1)S(1)} %select_n.91, s32[192,1536]{1,0:T(8,128)S(1)} %copy-done.2), kind=kOutput, calls=%fused_computation.3 | convolution fusion | flops 227672064 | bytes 2015232 | tf_op jit(solution)/shard_map/dot_general | solution.py:57
  19.5 0.0 copy-start.1
  19.5 0.3 fusion.16
  19.8 0.2 fusion.7
  20.0 0.1 constant_dynamic-slice_fusion.2
  20.1 0.1 copy-done.1
  20.2 0.2 fusion.10
  20.5 0.1 pad_maximum_fusion.6
  20.5 1.6 %collective-permute-start.2 = (f32[160,64]{0,1:T(8,128)S(1)}, f32[160,64]{0,1:T(8,128)S(1)}, u32[]{:S(2)}, u32[]{:S(2)}) collective-permute-start(f32[160,64]{0,1:T(8,128)S(1)} %pad_maximum_fusion.6), channel_id=1, source_target_pairs={{0,1},{1,0},{2,3},{3,2},{4,5},{5,4},{6,7},{7,6},{8,9},{9,8},{10,11... | collective-permute-start | bytes 122888 | tf_op jit(solution)/shard_map/ppermute | solution.py:65
  22.1 0.7 %reshape_reshape.3 = f32[8,2,96,64]{2,1,0,3:T(2,128)S(1)} reshape(f32[1536,64]{0,1:T(8,128)S(1)} %fusion.7) | data formatting | bytes 786432 | tf_op jit(solution)/shard_map/reshape;reshape | solution.py:77
  22.8 0.5 %constant_dynamic-slice_fusion.1 = (f32[8,1,96,64]{2,1,0,3:T(1,128)S(1)}, f32[8,1,96,64]{2,1,0,3:T(1,128)S(1)}) fusion(f32[8,2,96,64]{2,1,0,3:T(2,128)S(1)} %reshape_reshape.3, s32[]{:T(128)S(6)} %select_n.124, s32[]{:T(128)S(6)} %select_n.126), kind=kLoop, calls=%fused_computation.47 | loop fusion | bytes 786440 | tf_op jit(solution)/shard_map/jit(_take) | solution.py:79
  23.3 0.1 reshape.51
  23.4 1.5 %collective-permute-done.2 = f32[160,64]{0,1:T(8,128)S(1)} collective-permute-done((f32[160,64]{0,1:T(8,128)S(1)}, f32[160,64]{0,1:T(8,128)S(1)}, u32[]{:S(2)}, u32[]{:S(2)}) %collective-permute-start.2) | collective-permute-done | bytes 40992 | tf_op jit(solution)/shard_map/ppermute | solution.py:65
  24.9 0.1 slice_add_fusion.5
  25.0 0.1 collective-permute-start.3
  25.1 1.4 %collective-permute-done.3 = f32[832,64]{0,1:T(8,128)S(1)} collective-permute-done((f32[832,64]{0,1:T(8,128)S(1)}, f32[832,64]{0,1:T(8,128)S(1)}, u32[]{:S(2)}, u32[]{:S(2)}) %collective-permute-start.3) | collective-permute-done | bytes 213024 | tf_op jit(solution)/shard_map/ppermute | solution.py:82
  26.5 0.1 reshape.52
  26.7 0.1 fusion.3
  26.8 0.1 copy.29
  26.9 0.1 reshape.54
  27.1 0.3 collective-permute-start.4
  27.4 5.3 %collective-permute-done.4 = f32[448,64]{0,1:T(8,128)S(1)} collective-permute-done((f32[448,64]{0,1:T(8,128)S(1)}, f32[448,64]{0,1:T(8,128)S(1)}, u32[]{:S(2)}, u32[]{:S(2)}) %collective-permute-start.4) | collective-permute-done | bytes 114720 | tf_op jit(solution)/shard_map/ppermute | solution.py:82
  32.7 0.1 reshape.55
  32.9 0.1 pad_maximum_fusion.5
  33.0 0.6 %collective-permute-start.7 = (f32[160,64]{0,1:T(8,128)S(1)}, f32[160,64]{0,1:T(8,128)S(1)}, u32[]{:S(2)}, u32[]{:S(2)}) collective-permute-start(f32[160,64]{0,1:T(8,128)S(1)} %get-tuple-element.52), channel_id=1, source_target_pairs={{0,24},{2,26},{4,28},{6,30},{8,16},{10,18},{12,20},{14,22},{16,8},... | collective-permute-start | bytes 122888 | tf_op jit(solution)/shard_map/ppermute | solution.py:92
  33.6 0.9 %convolution_multiply_fusion = f32[96,64]{0,1:T(8,128)} fusion(f32[64,64]{1,0:T(8,128)S(1)} %copy-done, f32[160,64]{0,1:T(8,128)S(1)} %collective-permute-done.2, f32[192,64]{0,1:T(8,128)S(1)} %fusion.16, s32[]{:T(128)S(6)} %select_n.92), kind=kOutput, calls=%fused_computation.4 | convolution fusion | flops 4730880 | bytes 122884 | tf_op jit(solution)/shard_map/dot_general | solution.py:104
  34.5 0.8 %collective-permute-start.6 = (f32[160,64]{0,1:T(8,128)S(1)}, f32[160,64]{0,1:T(8,128)S(1)}, u32[]{:S(2)}, u32[]{:S(2)}) collective-permute-start(f32[160,64]{0,1:T(8,128)S(1)} %get-tuple-element.51), channel_id=1, source_target_pairs={{0,16},{2,18},{4,20},{6,22},{8,24},{10,26},{12,28},{14,30},{16,0},... | collective-permute-start | bytes 122888 | tf_op jit(solution)/shard_map/ppermute | solution.py:92
  35.2 3.1 %collective-permute-start.5 = (f32[160,64]{0,1:T(8,128)S(1)}, f32[160,64]{0,1:T(8,128)S(1)}, u32[]{:S(2)}, u32[]{:S(2)}) collective-permute-start(f32[160,64]{0,1:T(8,128)S(1)} %get-tuple-element.50), channel_id=1, source_target_pairs={{0,8},{2,10},{4,12},{6,14},{8,0},{10,2},{12,4},{14,6},{16,24},{18,... | collective-permute-start | bytes 122888 | tf_op jit(solution)/shard_map/ppermute | solution.py:92
  38.3 1.5 %collective-permute-done.7 = f32[160,64]{0,1:T(8,128)S(1)} collective-permute-done((f32[160,64]{0,1:T(8,128)S(1)}, f32[160,64]{0,1:T(8,128)S(1)}, u32[]{:S(2)}, u32[]{:S(2)}) %collective-permute-start.7) | collective-permute-done | bytes 40992 | tf_op jit(solution)/shard_map/ppermute | solution.py:92
  39.8 0.1 slice_bitcast_fusion
  39.9 1.3 %collective-permute-done.6 = f32[160,64]{0,1:T(8,128)S(1)} collective-permute-done((f32[160,64]{0,1:T(8,128)S(1)}, f32[160,64]{0,1:T(8,128)S(1)}, u32[]{:S(2)}, u32[]{:S(2)}) %collective-permute-start.6) | collective-permute-done | bytes 40992 | tf_op jit(solution)/shard_map/ppermute | solution.py:92
  41.1 0.1 slice_bitcast_fusion.1
  41.2 0.1 collective-permute-done.5
  41.3 0.1 slice_bitcast_fusion.2
  41.4 0.6 %gather_fusion = f32[4,64,64]{1,2,0:T(8,128)S(1)} fusion(f32[4,64,64]{1,2,0:T(8,128)S(1)} %pad_maximum_fusion.2, s32[1024]{0:T(1024)S(1)} %pad_clamp_fusion), kind=kCustom, calls=%fused_computation | custom fusion | bytes 131088 | tf_op jit(solution)/shard_map/jit(_take)/gather | solution.py:95
  41.9 0.1 select_reduce_fusion
  42.0 0.7 %copy.31 = f32[64,64]{1,0:T(8,128)} copy(f32[64,64]{0,1:T(8,128)S(1)} %broadcast_multiply_fusion) | data formatting | bytes 32768
  42.7 0.6 %fusion.6 = f32[96,64]{0,1:T(8,128)} fusion(f32[160,64]{0,1:T(8,128)S(1)} %collective-permute-done.7, f32[160,64]{0,1:T(8,128)S(1)} %collective-permute-done.6, f32[160,64]{0,1:T(8,128)S(1)} %collective-permute-done.5, f32[4,96,64]{1,2,0:T(8,128)S(1)} %fusion.5, s32[]{:T(128)S(6)} %select_n.132, pred[]{:T(512)S(6)} %and.66), kind=kLoop, calls=%fused_computation.26 | loop fusion | flops 30720 | bytes 122885 | tf_op jit(solution)/shard_map/mul | solution.py:105
  (15 shorter events, 0.2 us)
Async XLA Ops:
  0.6 16.1 %copy-start = (f32[64,64]{1,0:T(8,128)S(1)}, f32[64,64]{1,0:T(8,128)}, u32[]{:S(2)}) copy-start(f32[64,64]{1,0:T(8,128)} %param.13) | copy-start | bytes 49156
  0.6 18.1 %copy-start.2 = (s32[192,1536]{1,0:T(8,128)S(1)}, s32[192,1536]{1,0:T(8,128)}, u32[]{:S(2)}) copy-start(s32[192,1536]{1,0:T(8,128)} %param.10) | copy-start | bytes 3538948
  2.1 14.6 %all-to-all-start = ((bf16[8,96,64]{1,2,0:T(8,128)(2,1)}), bf16[8,96,64]{1,2,0:T(8,128)(2,1)S(1)}, u32[]{:S(2)}, u32[]{:S(2)}) async-start(bf16[8,96,64]{1,2,0:T(8,128)(2,1)} %broadcast_in_dim.43), calls=%async_computation | async-start | bytes 262144 | tf_op jit(solution)/shard_map/all_to_all | solution.py:50
  9.4 7.3 %collective-permute-start = (bf16[96,64]{0,1:T(8,128)(2,1)}, bf16[96,64]{0,1:T(8,128)(2,1)S(1)}, u32[]{:S(2)}, u32[]{:S(2)}) collective-permute-start(bf16[96,64]{0,1:T(8,128)(2,1)} %param.11), channel_id=1, source_target_pairs={{0,1},{1,0},{2,3},{3,2},{4,5},{5,4},{6,7},{7,6},{8,9},{9,8},{10,11... | collective-permute-start | bytes 36872 | tf_op jit(solution)/shard_map/ppermute | solution.py:44
  16.7 1.3 %collective-permute-start.1 = (bf16[8,96,64]{1,2,0:T(8,128)(2,1)S(1)}, bf16[8,96,64]{1,2,0:T(8,128)(2,1)S(1)}, u32[]{:S(2)}, u32[]{:S(2)}) collective-permute-start(bf16[8,96,64]{1,2,0:T(8,128)(2,1)S(1)} %all-to-all-done), channel_id=1, source_target_pairs={{0,2},{2,0},{1,3},{3,1},{4,6},{6,4},{5,7},{7,5},{8,10},{10,8},{9,1... | collective-permute-start | bytes 294920 | tf_op jit(solution)/shard_map/ppermute | solution.py:51
  19.5 0.7 %copy-start.1 = (bf16[96,64]{0,1:T(8,128)(2,1)S(1)}, bf16[96,64]{0,1:T(8,128)(2,1)}, u32[]{:S(2)}) copy-start(bf16[96,64]{0,1:T(8,128)(2,1)} %param.11) | copy-start | bytes 36868
  20.5 4.3 %collective-permute-start.2 = (f32[160,64]{0,1:T(8,128)S(1)}, f32[160,64]{0,1:T(8,128)S(1)}, u32[]{:S(2)}, u32[]{:S(2)}) collective-permute-start(f32[160,64]{0,1:T(8,128)S(1)} %pad_maximum_fusion.6), channel_id=1, source_target_pairs={{0,1},{1,0},{2,3},{3,2},{4,5},{5,4},{6,7},{7,6},{8,9},{9,8},{10,11... | collective-permute-start | bytes 122888 | tf_op jit(solution)/shard_map/ppermute | solution.py:65
  25.0 1.6 %collective-permute-start.3 = (f32[832,64]{0,1:T(8,128)S(1)}, f32[832,64]{0,1:T(8,128)S(1)}, u32[]{:S(2)}, u32[]{:S(2)}) collective-permute-start(f32[832,64]{0,1:T(8,128)S(1)} %pad_maximum_fusion), channel_id=1, source_target_pairs={{0,2},{2,0},{4,6},{6,4},{8,10},{10,8},{12,14},{14,12},{16,18},{18,... | collective-permute-start | bytes 638984 | tf_op jit(solution)/shard_map/ppermute | solution.py:82
  27.1 5.6 %collective-permute-start.4 = (f32[448,64]{0,1:T(8,128)S(1)}, f32[448,64]{0,1:T(8,128)S(1)}, u32[]{:S(2)}, u32[]{:S(2)}) collective-permute-start(f32[448,64]{0,1:T(8,128)S(1)} %pad_maximum_fusion.1), channel_id=1, source_target_pairs={{0,4},{2,6},{4,0},{6,2},{8,12},{10,14},{12,8},{14,10},{16,20},{18,... | collective-permute-start | bytes 344072 | tf_op jit(solution)/shard_map/ppermute | solution.py:82
  33.0 6.8 %collective-permute-start.7 = (f32[160,64]{0,1:T(8,128)S(1)}, f32[160,64]{0,1:T(8,128)S(1)}, u32[]{:S(2)}, u32[]{:S(2)}) collective-permute-start(f32[160,64]{0,1:T(8,128)S(1)} %get-tuple-element.52), channel_id=1, source_target_pairs={{0,24},{2,26},{4,28},{6,30},{8,16},{10,18},{12,20},{14,22},{16,8},... | collective-permute-start | bytes 122888 | tf_op jit(solution)/shard_map/ppermute | solution.py:92
  34.5 6.6 %collective-permute-start.6 = (f32[160,64]{0,1:T(8,128)S(1)}, f32[160,64]{0,1:T(8,128)S(1)}, u32[]{:S(2)}, u32[]{:S(2)}) collective-permute-start(f32[160,64]{0,1:T(8,128)S(1)} %get-tuple-element.51), channel_id=1, source_target_pairs={{0,16},{2,18},{4,20},{6,22},{8,24},{10,26},{12,28},{14,30},{16,0},... | collective-permute-start | bytes 122888 | tf_op jit(solution)/shard_map/ppermute | solution.py:92
  35.2 6.0 %collective-permute-start.5 = (f32[160,64]{0,1:T(8,128)S(1)}, f32[160,64]{0,1:T(8,128)S(1)}, u32[]{:S(2)}, u32[]{:S(2)}) collective-permute-start(f32[160,64]{0,1:T(8,128)S(1)} %get-tuple-element.50), channel_id=1, source_target_pairs={{0,8},{2,10},{4,12},{6,14},{8,0},{10,2},{12,4},{14,6},{16,24},{18,... | collective-permute-start | bytes 122888 | tf_op jit(solution)/shard_map/ppermute | solution.py:92

commit v5 on v4

--- a/solution.py
+++ b/solution.py
@@ -58,7 +58,7 @@
     ratio = (1.0 - counts.astype(jnp.float32) / rate).astype(jnp.bfloat16)
     gphi = jnp.dot(ratio, members, preferred_element_type=jnp.float32)
     gcol = lax.dot_general(ratio, factor_half, (((0,), (0,)), ((), ())), preferred_element_type=jnp.float32)
-    part = jnp.dot(theta_wide.T, gphi, precision=HI)
+    part = lax.dot_general(gphi, theta_wide, (((0,), (0,)), ((), ())), precision=HI)
     mc = gphi.shape[0] // nc
     if nc == 2:
         send = jnp.concatenate([lax.dynamic_slice_in_dim(gphi, (1 - c) * mc, mc), part])
@@ -92,7 +92,7 @@
             got = lax.ppermute(send, ROW, [(i, i ^ (s * b)) for i in range(nr)])
             total = total + got[:mr]
             held.append(got[mr:])
-        part_sum = jnp.sum(jnp.take(jnp.stack(held), quad ^ jnp.arange(4), axis=0), axis=0)
+        part_sum = (held[0] + held[1]) + (held[2] + held[3])
         acc = total[None]
     elif acc.shape[0] == 2:
         mine = (r // b) % 2
@@ -103,7 +103,7 @@
     phi_sum = acc[0]
     theta_grad = inverse * jnp.dot(gphi_sum, affinity.T, precision=HI)
     phi_grad = inverse * phi_sum
-    affinity_grad = inverse * inverse * part_sum
+    affinity_grad = inverse * inverse * part_sum.T
     return (theta_grad, phi_grad, affinity_grad)
 
 

time: 44 us -> 42.8 us (0.973)
  local copies, waits for them, and re-layouts: 5.41 us -> 3.94 us
  other arithmetic: 1.32 us -> 1.92 us
    mul x1, other arithmetic: 0.01 us -> 0.71 us  [shards(): affinity_grad = inverse * inverse * part_sum.T]
    unnamed x7 -> x6, local copies, waits for them, and re-layouts: 0.81 us -> 0.11 us
    gather x1 -> x0, local copies, waits for them, and re-layouts: 0.56 us -> none  [shards(): jnp.take(jnp.stack(held), quad ^ jnp.arange(4), axis=0)]
  transfers between devices with their start and end apart: 9 -> 9, of which waited for: 8 -> 7; matrix products, arithmetic and copies ran while one was open for 8% -> 8% of each run, Pallas kernels for 0% -> 0%
where the time goes in v5:
time: 42.8 us; the launch traced here: 42.2 us
  waiting for transfers between devices  16.8 us (39%)
  starting transfers between devices  15.2 us (36%)
  local copies, waits for them, and re-layouts  3.94 us (9%)
  matrix products  3.39 us (8%)
  other arithmetic  1.92 us (4%)
  between operations  0.93 us (2%)
    all_to_all x1, starting transfers between devices, shards(): lax.all_to_all(jnp.broadcast_to(phi[None], (nchip,) + phi.shape), 'chip',...  7.25 us
    ppermute x2, waiting for transfers between devices, shards(): got = lax.ppermute(send, ROW, [(i, i ^ b) for i in range(nr)])  6.75 us
    all_to_all x1, waiting for transfers between devices, shards(): lax.all_to_all(jnp.broadcast_to(phi[None], (nchip,) + phi.shape), 'chip',...  5.82 us
    ppermute x3, starting transfers between devices, shards(): got = lax.ppermute(send, ROW, [(i, i ^ s * b) for i in range(nr)])  4.45 us
    ppermute x3, waiting for transfers between devices, shards(): got = lax.ppermute(send, ROW, [(i, i ^ s * b) for i in range(nr)])  2.54 us
    ppermute x1, starting transfers between devices, shards(): got = lax.ppermute(send, 'col', SWAP)  1.58 us
    ppermute x1, starting transfers between devices, shards(): other = lax.ppermute(theta, 'col', SWAP)  1.52 us
    broadcast_in_dim x1, local copies, waits for them, and re-layouts, shards(): jnp.broadcast_to(phi[None], (nchip,) + phi.shape)  1.49 us
  transfers between devices with their start and end apart: 9, of which 7 were waited for; matrix products, arithmetic and copies ran while one was open for 8% of the time, Pallas kernels for 0%

profile of v5, /device:TPU:0, one launch (start us, length us, event | category | flops | bytes accessed | tf_op | source)
XLA Modules:
  0.0 42.2 jit_solution(12078909274785135777)
XLA Ops:
  0.6 0.0 copy-start
  0.6 0.0 copy-start.2
  0.7 1.5 %broadcast_in_dim.33 = bf16[8,96,64]{1,2,0:T(8,128)(2,1)} broadcast(bf16[96,64]{0,1:T(8,128)(2,1)} %param.12), dimensions={1,2} | broadcast | bytes 110592 | tf_op jit(solution)/shard_map/broadcast_in_dim | solution.py:50
  2.1 7.3 %all-to-all-start = ((bf16[8,96,64]{1,2,0:T(8,128)(2,1)}), bf16[8,96,64]{1,2,0:T(8,128)(2,1)S(1)}, u32[]{:S(2)}, u32[]{:S(2)}) async-start(bf16[8,96,64]{1,2,0:T(8,128)(2,1)} %broadcast_in_dim.33), calls=%async_computation | async-start | bytes 262144 | tf_op jit(solution)/shard_map/all_to_all | solution.py:50
  9.4 1.5 %collective-permute-start = (bf16[96,64]{0,1:T(8,128)(2,1)}, bf16[96,64]{0,1:T(8,128)(2,1)S(1)}, u32[]{:S(2)}, u32[]{:S(2)}) collective-permute-start(bf16[96,64]{0,1:T(8,128)(2,1)} %param.11), channel_id=1, source_target_pairs={{0,1},{1,0},{2,3},{3,2},{4,5},{5,4},{6,7},{7,6},{8,9},{9,8},{10,11... | collective-permute-start | bytes 36872 | tf_op jit(solution)/shard_map/ppermute | solution.py:44
  10.9 5.8 %all-to-all-done = bf16[8,96,64]{1,2,0:T(8,128)(2,1)S(1)} async-done(((bf16[8,96,64]{1,2,0:T(8,128)(2,1)}), bf16[8,96,64]{1,2,0:T(8,128)(2,1)S(1)}, u32[]{:S(2)}, u32[]{:S(2)}) %all-to-all-start) | async-done | bytes 98336 | tf_op jit(solution)/shard_map/all_to_all | solution.py:50
  16.7 0.0 collective-permute-start.1
  16.7 0.0 collective-permute-done
  16.7 0.0 copy-done
  16.8 1.1 %fusion.14 = f32[192,64]{0,1:T(8,128)S(1)} fusion(f32[64,64]{1,0:T(8,128)S(1)} %copy-done, bf16[96,64]{0,1:T(8,128)(2,1)S(1)} %collective-permute-done, bf16[96,64]{0,1:T(8,128)(2,1)} %param.11, pred[]{:T(512)S(6)} %eq.10), kind=kOutput, calls=%fused_computation.40 | convolution fusion | flops 9547776 | bytes 90113 | tf_op jit(solution)/shard_map/dot_general | solution.py:55
  17.8 0.3 collective-permute-done.1
  18.1 0.1 maximum_select_fusion
  18.2 0.3 copy.23
  18.5 0.3 select_n.71
  18.7 0.0 copy-done.2
  18.7 0.7 %fusion.1 = bf16[192,1536]{1,0:T(8,128)(2,1)S(1)} fusion(f32[192,64]{0,1:T(8,128)S(1)} %fusion.14, bf16[1536,64]{0,1:T(8,128)(2,1)S(1)} %select_n.71, s32[192,1536]{1,0:T(8,128)S(1)} %copy-done.2), kind=kOutput, calls=%fused_computation.2 | convolution fusion | flops 227672064 | bytes 2015232 | tf_op jit(solution)/shard_map/dot_general | solution.py:57
  19.5 0.0 copy-start.1
  19.5 0.3 fusion.18
  19.8 0.2 fusion.10
  20.0 0.1 constant_dynamic-slice_fusion.2
  20.1 0.1 copy-done.1
  20.2 0.2 fusion.13
  20.4 0.1 pad_maximum_fusion.5
  20.5 1.6 %collective-permute-start.2 = (f32[160,64]{0,1:T(8,128)S(1)}, f32[160,64]{0,1:T(8,128)S(1)}, u32[]{:S(2)}, u32[]{:S(2)}) collective-permute-start(f32[160,64]{0,1:T(8,128)S(1)} %pad_maximum_fusion.5), channel_id=1, source_target_pairs={{0,1},{1,0},{2,3},{3,2},{4,5},{5,4},{6,7},{7,6},{8,9},{9,8},{10,11... | collective-permute-start | bytes 122888 | tf_op jit(solution)/shard_map/ppermute | solution.py:65
  22.1 0.7 %reshape_reshape.3 = f32[8,2,96,64]{2,1,0,3:T(2,128)S(1)} reshape(f32[1536,64]{0,1:T(8,128)S(1)} %fusion.10) | data formatting | bytes 786432 | tf_op jit(solution)/shard_map/reshape;reshape | solution.py:77
  22.8 0.5 %constant_dynamic-slice_fusion.1 = (f32[8,1,96,64]{2,1,0,3:T(1,128)S(1)}, f32[8,1,96,64]{2,1,0,3:T(1,128)S(1)}) fusion(f32[8,2,96,64]{2,1,0,3:T(2,128)S(1)} %reshape_reshape.3, s32[]{:T(128)S(6)} %select_n.101, s32[]{:T(128)S(6)} %select_n.103), kind=kLoop, calls=%fused_computation.42 | loop fusion | bytes 786440 | tf_op jit(solution)/shard_map/jit(_take) | solution.py:79
  23.3 0.1 reshape.30
  23.4 1.5 %collective-permute-done.2 = f32[160,64]{0,1:T(8,128)S(1)} collective-permute-done((f32[160,64]{0,1:T(8,128)S(1)}, f32[160,64]{0,1:T(8,128)S(1)}, u32[]{:S(2)}, u32[]{:S(2)}) %collective-permute-start.2) | collective-permute-done | bytes 40992 | tf_op jit(solution)/shard_map/ppermute | solution.py:65
  24.9 0.1 slice_add_fusion.7
  25.0 0.1 collective-permute-start.3
  25.1 1.4 %collective-permute-done.3 = f32[832,64]{0,1:T(8,128)S(1)} collective-permute-done((f32[832,64]{0,1:T(8,128)S(1)}, f32[832,64]{0,1:T(8,128)S(1)}, u32[]{:S(2)}, u32[]{:S(2)}) %collective-permute-start.3) | collective-permute-done | bytes 213024 | tf_op jit(solution)/shard_map/ppermute | solution.py:82
  26.5 0.1 reshape.31
  26.7 0.1 fusion.3
  26.8 0.1 copy.28
  26.9 0.1 reshape.33
  27.1 0.3 collective-permute-start.4
  27.3 5.3 %collective-permute-done.4 = f32[448,64]{0,1:T(8,128)S(1)} collective-permute-done((f32[448,64]{0,1:T(8,128)S(1)}, f32[448,64]{0,1:T(8,128)S(1)}, u32[]{:S(2)}, u32[]{:S(2)}) %collective-permute-start.4) | collective-permute-done | bytes 114720 | tf_op jit(solution)/shard_map/ppermute | solution.py:82
  32.7 0.1 reshape.34
  32.9 0.1 pad_maximum_fusion.4
  33.0 0.6 %collective-permute-start.7 = (f32[160,64]{0,1:T(8,128)S(1)}, f32[160,64]{0,1:T(8,128)S(1)}, u32[]{:S(2)}, u32[]{:S(2)}) collective-permute-start(f32[160,64]{0,1:T(8,128)S(1)} %get-tuple-element.46), channel_id=1, source_target_pairs={{0,24},{2,26},{4,28},{6,30},{8,16},{10,18},{12,20},{14,22},{16,8},... | collective-permute-start | bytes 122888 | tf_op jit(solution)/shard_map/ppermute | solution.py:92
  33.6 0.8 %collective-permute-start.6 = (f32[160,64]{0,1:T(8,128)S(1)}, f32[160,64]{0,1:T(8,128)S(1)}, u32[]{:S(2)}, u32[]{:S(2)}) collective-permute-start(f32[160,64]{0,1:T(8,128)S(1)} %get-tuple-element.45), channel_id=1, source_target_pairs={{0,16},{2,18},{4,20},{6,22},{8,24},{10,26},{12,28},{14,30},{16,0},... | collective-permute-start | bytes 122888 | tf_op jit(solution)/shard_map/ppermute | solution.py:92
  34.4 3.1 %collective-permute-start.5 = (f32[160,64]{0,1:T(8,128)S(1)}, f32[160,64]{0,1:T(8,128)S(1)}, u32[]{:S(2)}, u32[]{:S(2)}) collective-permute-start(f32[160,64]{0,1:T(8,128)S(1)} %get-tuple-element.44), channel_id=1, source_target_pairs={{0,8},{2,10},{4,12},{6,14},{8,0},{10,2},{12,4},{14,6},{16,24},{18,... | collective-permute-start | bytes 122888 | tf_op jit(solution)/shard_map/ppermute | solution.py:92
  37.4 0.9 %convolution_multiply_fusion = f32[96,64]{0,1:T(8,128)} fusion(f32[64,64]{1,0:T(8,128)S(1)} %copy-done, f32[160,64]{0,1:T(8,128)S(1)} %collective-permute-done.2, f32[192,64]{0,1:T(8,128)S(1)} %fusion.18, s32[]{:T(128)S(6)} %select_n.72), kind=kOutput, calls=%fused_computation.3 | convolution fusion | flops 4730880 | bytes 122884 | tf_op jit(solution)/shard_map/dot_general | solution.py:104
  38.3 1.4 %collective-permute-done.7 = f32[160,64]{0,1:T(8,128)S(1)} collective-permute-done((f32[160,64]{0,1:T(8,128)S(1)}, f32[160,64]{0,1:T(8,128)S(1)}, u32[]{:S(2)}, u32[]{:S(2)}) %collective-permute-start.7) | collective-permute-done | bytes 40992 | tf_op jit(solution)/shard_map/ppermute | solution.py:92
  39.7 1.2 %collective-permute-done.6 = f32[160,64]{0,1:T(8,128)S(1)} collective-permute-done((f32[160,64]{0,1:T(8,128)S(1)}, f32[160,64]{0,1:T(8,128)S(1)}, u32[]{:S(2)}, u32[]{:S(2)}) %collective-permute-start.6) | collective-permute-done | bytes 40992 | tf_op jit(solution)/shard_map/ppermute | solution.py:92
  40.8 0.0 collective-permute-done.5
  40.8 0.7 %fusion.8 = f32[64,64]{1,0:T(8,128)} fusion(f32[160,64]{0,1:T(8,128)S(1)} %collective-permute-done.7, f32[160,64]{0,1:T(8,128)S(1)} %collective-permute-done.6, f32[64,64]{0,1:T(8,128)S(1)} %slice_add_fusion.5, f32[160,64]{0,1:T(8,128)S(1)} %collective-permute-done.5), kind=kLoop, calls=%fused_computation.22 | loop fusion | flops 16384 | bytes 81920 | tf_op jit(solution)/shard_map/mul | solution.py:106
  41.6 0.6 %fusion.9 = f32[96,64]{0,1:T(8,128)} fusion(f32[160,64]{0,1:T(8,128)S(1)} %collective-permute-done.7, f32[160,64]{0,1:T(8,128)S(1)} %collective-permute-done.6, f32[160,64]{0,1:T(8,128)S(1)} %collective-permute-done.5, f32[4,96,64]{1,2,0:T(8,128)S(1)} %fusion.5, s32[]{:T(128)S(6)} %select_n.109, pred[]{:T(512)S(6)} %and.58), kind=kLoop, calls=%fused_computation.25 | loop fusion | flops 30720 | bytes 122885 | tf_op jit(solution)/shard_map/mul | solution.py:105
  (10 shorter events, 0.2 us)
Async XLA Ops:
  0.6 16.1 %copy-start = (f32[64,64]{1,0:T(8,128)S(1)}, f32[64,64]{1,0:T(8,128)}, u32[]{:S(2)}) copy-start(f32[64,64]{1,0:T(8,128)} %param.13) | copy-start | bytes 49156
  0.6 18.1 %copy-start.2 = (s32[192,1536]{1,0:T(8,128)S(1)}, s32[192,1536]{1,0:T(8,128)}, u32[]{:S(2)}) copy-start(s32[192,1536]{1,0:T(8,128)} %param.10) | copy-start | bytes 3538948
  2.1 14.6 %all-to-all-start = ((bf16[8,96,64]{1,2,0:T(8,128)(2,1)}), bf16[8,96,64]{1,2,0:T(8,128)(2,1)S(1)}, u32[]{:S(2)}, u32[]{:S(2)}) async-start(bf16[8,96,64]{1,2,0:T(8,128)(2,1)} %broadcast_in_dim.33), calls=%async_computation | async-start | bytes 262144 | tf_op jit(solution)/shard_map/all_to_all | solution.py:50
  9.4 7.3 %collective-permute-start = (bf16[96,64]{0,1:T(8,128)(2,1)}, bf16[96,64]{0,1:T(8,128)(2,1)S(1)}, u32[]{:S(2)}, u32[]{:S(2)}) collective-permute-start(bf16[96,64]{0,1:T(8,128)(2,1)} %param.11), channel_id=1, source_target_pairs={{0,1},{1,0},{2,3},{3,2},{4,5},{5,4},{6,7},{7,6},{8,9},{9,8},{10,11... | collective-permute-start | bytes 36872 | tf_op jit(solution)/shard_map/ppermute | solution.py:44
  16.7 1.3 %collective-permute-start.1 = (bf16[8,96,64]{1,2,0:T(8,128)(2,1)S(1)}, bf16[8,96,64]{1,2,0:T(8,128)(2,1)S(1)}, u32[]{:S(2)}, u32[]{:S(2)}) collective-permute-start(bf16[8,96,64]{1,2,0:T(8,128)(2,1)S(1)} %all-to-all-done), channel_id=1, source_target_pairs={{0,2},{2,0},{1,3},{3,1},{4,6},{6,4},{5,7},{7,5},{8,10},{10,8},{9,1... | collective-permute-start | bytes 294920 | tf_op jit(solution)/shard_map/ppermute | solution.py:51
  19.5 0.7 %copy-start.1 = (bf16[96,64]{0,1:T(8,128)(2,1)S(1)}, bf16[96,64]{0,1:T(8,128)(2,1)}, u32[]{:S(2)}) copy-start(bf16[96,64]{0,1:T(8,128)(2,1)} %param.11) | copy-start | bytes 36868
  20.5 4.3 %collective-permute-start.2 = (f32[160,64]{0,1:T(8,128)S(1)}, f32[160,64]{0,1:T(8,128)S(1)}, u32[]{:S(2)}, u32[]{:S(2)}) collective-permute-start(f32[160,64]{0,1:T(8,128)S(1)} %pad_maximum_fusion.5), channel_id=1, source_target_pairs={{0,1},{1,0},{2,3},{3,2},{4,5},{5,4},{6,7},{7,6},{8,9},{9,8},{10,11... | collective-permute-start | bytes 122888 | tf_op jit(solution)/shard_map/ppermute | solution.py:65
  25.0 1.6 %collective-permute-start.3 = (f32[832,64]{0,1:T(8,128)S(1)}, f32[832,64]{0,1:T(8,128)S(1)}, u32[]{:S(2)}, u32[]{:S(2)}) collective-permute-start(f32[832,64]{0,1:T(8,128)S(1)} %pad_maximum_fusion), channel_id=1, source_target_pairs={{0,2},{2,0},{4,6},{6,4},{8,10},{10,8},{12,14},{14,12},{16,18},{18,... | collective-permute-start | bytes 638984 | tf_op jit(solution)/shard_map/ppermute | solution.py:82
  27.1 5.6 %collective-permute-start.4 = (f32[448,64]{0,1:T(8,128)S(1)}, f32[448,64]{0,1:T(8,128)S(1)}, u32[]{:S(2)}, u32[]{:S(2)}) collective-permute-start(f32[448,64]{0,1:T(8,128)S(1)} %pad_maximum_fusion.1), channel_id=1, source_target_pairs={{0,4},{2,6},{4,0},{6,2},{8,12},{10,14},{12,8},{14,10},{16,20},{18,... | collective-permute-start | bytes 344072 | tf_op jit(solution)/shard_map/ppermute | solution.py:82
  33.0 6.7 %collective-permute-start.7 = (f32[160,64]{0,1:T(8,128)S(1)}, f32[160,64]{0,1:T(8,128)S(1)}, u32[]{:S(2)}, u32[]{:S(2)}) collective-permute-start(f32[160,64]{0,1:T(8,128)S(1)} %get-tuple-element.46), channel_id=1, source_target_pairs={{0,24},{2,26},{4,28},{6,30},{8,16},{10,18},{12,20},{14,22},{16,8},... | collective-permute-start | bytes 122888 | tf_op jit(solution)/shard_map/ppermute | solution.py:92
  33.6 7.2 %collective-permute-start.6 = (f32[160,64]{0,1:T(8,128)S(1)}, f32[160,64]{0,1:T(8,128)S(1)}, u32[]{:S(2)}, u32[]{:S(2)}) collective-permute-start(f32[160,64]{0,1:T(8,128)S(1)} %get-tuple-element.45), channel_id=1, source_target_pairs={{0,16},{2,18},{4,20},{6,22},{8,24},{10,26},{12,28},{14,30},{16,0},... | collective-permute-start | bytes 122888 | tf_op jit(solution)/shard_map/ppermute | solution.py:92
  34.4 6.5 %collective-permute-start.5 = (f32[160,64]{0,1:T(8,128)S(1)}, f32[160,64]{0,1:T(8,128)S(1)}, u32[]{:S(2)}, u32[]{:S(2)}) collective-permute-start(f32[160,64]{0,1:T(8,128)S(1)} %get-tuple-element.44), channel_id=1, source_target_pairs={{0,8},{2,10},{4,12},{6,14},{8,0},{10,2},{12,4},{14,6},{16,24},{18,... | collective-permute-start | bytes 122888 | tf_op jit(solution)/shard_map/ppermute | solution.py:92

commit v6 on v5

--- a/solution.py
+++ b/solution.py
@@ -60,7 +60,10 @@
     gcol = lax.dot_general(ratio, factor_half, (((0,), (0,)), ((), ())), preferred_element_type=jnp.float32)
     part = lax.dot_general(gphi, theta_wide, (((0,), (0,)), ((), ())), precision=HI)
     mc = gphi.shape[0] // nc
-    if nc == 2:
+    deferred = nc == 2 and nr >= 8
+    if deferred:
+        part_sum = part
+    elif nc == 2:
         send = jnp.concatenate([lax.dynamic_slice_in_dim(gphi, (1 - c) * mc, mc), part])
         got = lax.ppermute(send, "col", SWAP)
         gphi_sum = lax.dynamic_slice_in_dim(gphi, c * mc, mc) + got[:mc]
@@ -81,7 +84,15 @@
         send = jnp.concatenate([away.reshape(-1, k), part_sum])
         got = lax.ppermute(send, ROW, [(i, i ^ b) for i in range(nr)])
         acc = keep + got[: keep.shape[0] * mr].reshape(keep.shape)
-        part_sum = part_sum + got[keep.shape[0] * mr:]
+        if deferred and b == 2:
+            send = jnp.concatenate([lax.dynamic_slice_in_dim(gphi, (1 - c) * mc, mc), part_sum])
+            got_col = lax.ppermute(send, "col", SWAP)
+            got_diag = lax.ppermute(part_sum, ROW + ("col",), [(i, i ^ (2 * b + 1)) for i in range(nr * nc)])
+            gphi_sum = lax.dynamic_slice_in_dim(gphi, c * mc, mc) + got_col[:mc]
+            part_sum = (part_sum + got_col[mc:]) + (got[keep.shape[0] * mr:] + got_diag)
+            deferred = False
+        else:
+            part_sum = part_sum + got[keep.shape[0] * mr:]
         b *= 2
     if acc.shape[0] == 4:
         quad = (r // b) % 4

time: 42.8 us -> 41.2 us (0.963)
  waiting for transfers between devices: 16.8 us -> 13.3 us
  starting transfers between devices: 15.2 us -> 17.2 us
    ppermute x2, waiting for transfers between devices: 6.75 us -> 3.52 us  [shards(): got = lax.ppermute(send, ROW, [(i, i ^ b) for i in range(nr)])]
    ppermute x1 -> x2, starting transfers between devices: 1.58 us -> 3.35 us  [the longest x1 2.78 us: shards(): lax.ppermute(part_sum, ROW + ('col',), [(i, i ^ 2 * b + 1) for i in range...]
    ppermute x3, waiting for transfers between devices: 2.54 us -> 2.07 us  [shards(): got = lax.ppermute(send, ROW, [(i, i ^ s * b) for i in range(nr)])]
    ppermute x1 -> x2, waiting for transfers between devices: 1.46 us -> 1.63 us  [the longest x1 1.21 us: shards(): lax.ppermute(part_sum, ROW + ('col',), [(i, i ^ 2 * b + 1) for i in range...]
  transfers between devices with their start and end apart: 9 -> 10, of which waited for: 7 -> 8; matrix products, arithmetic and copies ran while one was open for 8% -> 6% of each run, Pallas kernels for 0% -> 0%
where the time goes in v6:
time: 41.2 us; the launch traced here: 40.6 us
  starting transfers between devices  17.2 us (42%)
  waiting for transfers between devices  13.3 us (32%)
  local copies, waits for them, and re-layouts  3.93 us (10%)
  matrix products  3.4 us (8%)
  other arithmetic  1.91 us (5%)
  between operations  0.86 us (2%)
    all_to_all x1, starting transfers between devices, shards(): lax.all_to_all(jnp.broadcast_to(phi[None], (nchip,) + phi.shape), 'chip',...  7.25 us
    all_to_all x1, waiting for transfers between devices, shards(): lax.all_to_all(jnp.broadcast_to(phi[None], (nchip,) + phi.shape), 'chip',...  5.82 us
    ppermute x3, starting transfers between devices, shards(): got = lax.ppermute(send, ROW, [(i, i ^ s * b) for i in range(nr)])  4.45 us
    ppermute x2, waiting for transfers between devices, shards(): got = lax.ppermute(send, ROW, [(i, i ^ b) for i in range(nr)])  3.52 us
    ppermute x1, starting transfers between devices, shards(): lax.ppermute(part_sum, ROW + ('col',), [(i, i ^ 2 * b + 1) for i in range...  2.78 us
    ppermute x3, waiting for transfers between devices, shards(): got = lax.ppermute(send, ROW, [(i, i ^ s * b) for i in range(nr)])  2.07 us
    ppermute x1, starting transfers between devices, shards(): other = lax.ppermute(theta, 'col', SWAP)  1.52 us
    broadcast_in_dim x1, local copies, waits for them, and re-layouts, shards(): jnp.broadcast_to(phi[None], (nchip,) + phi.shape)  1.49 us
  transfers between devices with their start and end apart: 10, of which 8 were waited for; matrix products, arithmetic and copies ran while one was open for 6% of the time, Pallas kernels for 0%

profile of v6, /device:TPU:0, one launch (start us, length us, event | category | flops | bytes accessed | tf_op | source)
XLA Modules:
  0.0 40.6 jit_solution(8132168195741689228)
XLA Ops:
  0.6 0.0 copy-start
  0.6 0.0 copy-start.2
  0.7 1.5 %broadcast_in_dim.33 = bf16[8,96,64]{1,2,0:T(8,128)(2,1)} broadcast(bf16[96,64]{0,1:T(8,128)(2,1)} %param.12), dimensions={1,2} | broadcast | bytes 110592 | tf_op jit(solution)/shard_map/broadcast_in_dim | solution.py:50
  2.1 7.3 %all-to-all-start = ((bf16[8,96,64]{1,2,0:T(8,128)(2,1)}), bf16[8,96,64]{1,2,0:T(8,128)(2,1)S(1)}, u32[]{:S(2)}, u32[]{:S(2)}) async-start(bf16[8,96,64]{1,2,0:T(8,128)(2,1)} %broadcast_in_dim.33), calls=%async_computation | async-start | bytes 262144 | tf_op jit(solution)/shard_map/all_to_all | solution.py:50
  9.4 1.5 %collective-permute-start = (bf16[96,64]{0,1:T(8,128)(2,1)}, bf16[96,64]{0,1:T(8,128)(2,1)S(1)}, u32[]{:S(2)}, u32[]{:S(2)}) collective-permute-start(bf16[96,64]{0,1:T(8,128)(2,1)} %param.11), channel_id=1, source_target_pairs={{0,1},{1,0},{2,3},{3,2},{4,5},{5,4},{6,7},{7,6},{8,9},{9,8},{10,11... | collective-permute-start | bytes 36872 | tf_op jit(solution)/shard_map/ppermute | solution.py:44
  10.9 5.8 %all-to-all-done = bf16[8,96,64]{1,2,0:T(8,128)(2,1)S(1)} async-done(((bf16[8,96,64]{1,2,0:T(8,128)(2,1)}), bf16[8,96,64]{1,2,0:T(8,128)(2,1)S(1)}, u32[]{:S(2)}, u32[]{:S(2)}) %all-to-all-start) | async-done | bytes 98336 | tf_op jit(solution)/shard_map/all_to_all | solution.py:50
  16.7 0.0 collective-permute-start.1
  16.7 0.0 collective-permute-done
  16.7 0.0 copy-done
  16.8 1.1 %fusion.15 = f32[192,64]{0,1:T(8,128)S(1)} fusion(f32[64,64]{1,0:T(8,128)S(1)} %copy-done, bf16[96,64]{0,1:T(8,128)(2,1)S(1)} %collective-permute-done, bf16[96,64]{0,1:T(8,128)(2,1)} %param.11, pred[]{:T(512)S(6)} %eq.10), kind=kOutput, calls=%fused_computation.41 | convolution fusion | flops 9547776 | bytes 90113 | tf_op jit(solution)/shard_map/dot_general | solution.py:55
  17.8 0.3 collective-permute-done.1
  18.1 0.1 maximum_select_fusion
  18.2 0.3 copy.23
  18.5 0.3 select_n.71
  18.7 0.0 copy-done.2
  18.7 0.7 %fusion.1 = bf16[192,1536]{1,0:T(8,128)(2,1)S(1)} fusion(f32[192,64]{0,1:T(8,128)S(1)} %fusion.15, bf16[1536,64]{0,1:T(8,128)(2,1)S(1)} %select_n.71, s32[192,1536]{1,0:T(8,128)S(1)} %copy-done.2), kind=kOutput, calls=%fused_computation.2 | convolution fusion | flops 227672064 | bytes 2015232 | tf_op jit(solution)/shard_map/dot_general | solution.py:57
  19.5 0.3 fusion.19
  19.8 0.2 fusion.11
  20.0 0.7 %reshape_reshape.3 = f32[8,2,96,64]{2,1,0,3:T(2,128)S(1)} reshape(f32[1536,64]{0,1:T(8,128)S(1)} %fusion.11) | data formatting | bytes 786432 | tf_op jit(solution)/shard_map/reshape;reshape | solution.py:80
  20.7 0.0 copy-start.1
  20.7 0.5 %constant_dynamic-slice_fusion = (f32[8,1,96,64]{2,1,0,3:T(1,128)S(1)}, f32[8,1,96,64]{2,1,0,3:T(1,128)S(1)}) fusion(f32[8,2,96,64]{2,1,0,3:T(2,128)S(1)} %reshape_reshape.3, s32[]{:T(128)S(6)} %select_n.103, s32[]{:T(128)S(6)} %select_n.101), kind=kLoop, calls=%fused_computation.42 | loop fusion | bytes 786440 | tf_op jit(solution)/shard_map/jit(_take) | solution.py:82
  21.2 0.1 reshape.30
  21.3 0.1 copy-done.1
  21.4 0.2 fusion.14
  21.7 0.3 collective-permute-start.2
  22.0 1.2 %collective-permute-done.2 = f32[832,64]{0,1:T(8,128)S(1)} collective-permute-done((f32[832,64]{0,1:T(8,128)S(1)}, f32[832,64]{0,1:T(8,128)S(1)}, u32[]{:S(2)}, u32[]{:S(2)}) %collective-permute-start.2) | collective-permute-done | bytes 213024 | tf_op jit(solution)/shard_map/ppermute | solution.py:85
  23.2 0.1 reshape.31
  23.4 0.1 fusion.3
  23.5 0.1 copy.28
  23.6 0.1 reshape.33
  23.8 0.3 collective-permute-start.4
  24.1 0.1 constant_dynamic-slice_fusion.2
  24.1 2.8 %collective-permute-start.5 = (f32[64,64]{0,1:T(8,128)S(1)}, f32[64,64]{0,1:T(8,128)S(1)}, u32[]{:S(2)}, u32[]{:S(2)}) collective-permute-start(f32[64,64]{0,1:T(8,128)S(1)} %slice_add_fusion.9), channel_id=1, source_target_pairs={{0,5},{1,4},{2,7},{3,6},{4,1},{5,0},{6,3},{7,2},{8,13},{9,12},{10,... | collective-permute-start | bytes 49160 | tf_op jit(solution)/shard_map/ppermute | solution.py:90
  26.9 0.1 pad_maximum_fusion.5
  27.0 0.6 %collective-permute-start.3 = (f32[160,64]{0,1:T(8,128)S(1)}, f32[160,64]{0,1:T(8,128)S(1)}, u32[]{:S(2)}, u32[]{:S(2)}) collective-permute-start(f32[160,64]{0,1:T(8,128)S(1)} %pad_maximum_fusion.5), channel_id=1, source_target_pairs={{0,1},{1,0},{2,3},{3,2},{4,5},{5,4},{6,7},{7,6},{8,9},{9,8},{10,11... | collective-permute-start | bytes 122888 | tf_op jit(solution)/shard_map/ppermute | solution.py:89
  27.6 2.3 %collective-permute-done.4 = f32[448,64]{0,1:T(8,128)S(1)} collective-permute-done((f32[448,64]{0,1:T(8,128)S(1)}, f32[448,64]{0,1:T(8,128)S(1)}, u32[]{:S(2)}, u32[]{:S(2)}) %collective-permute-start.4) | collective-permute-done | bytes 114720 | tf_op jit(solution)/shard_map/ppermute | solution.py:85
  29.9 0.1 reshape.34
  30.1 1.2 %collective-permute-done.5 = f32[64,64]{0,1:T(8,128)S(1)} collective-permute-done((f32[64,64]{0,1:T(8,128)S(1)}, f32[64,64]{0,1:T(8,128)S(1)}, u32[]{:S(2)}, u32[]{:S(2)}) %collective-permute-start.5) | collective-permute-done | bytes 16416 | tf_op jit(solution)/shard_map/ppermute | solution.py:90
  31.3 0.4 %collective-permute-done.3 = f32[160,64]{0,1:T(8,128)S(1)} collective-permute-done((f32[160,64]{0,1:T(8,128)S(1)}, f32[160,64]{0,1:T(8,128)S(1)}, u32[]{:S(2)}, u32[]{:S(2)}) %collective-permute-start.3) | collective-permute-done | bytes 40992 | tf_op jit(solution)/shard_map/ppermute | solution.py:89
  31.7 0.1 fusion.10
  31.8 0.1 pad_maximum_fusion.4
  31.9 0.6 %collective-permute-start.8 = (f32[160,64]{0,1:T(8,128)S(1)}, f32[160,64]{0,1:T(8,128)S(1)}, u32[]{:S(2)}, u32[]{:S(2)}) collective-permute-start(f32[160,64]{0,1:T(8,128)S(1)} %get-tuple-element.46), channel_id=1, source_target_pairs={{0,24},{2,26},{4,28},{6,30},{8,16},{10,18},{12,20},{14,22},{16,8},... | collective-permute-start | bytes 122888 | tf_op jit(solution)/shard_map/ppermute | solution.py:103
  32.5 0.8 %collective-permute-start.7 = (f32[160,64]{0,1:T(8,128)S(1)}, f32[160,64]{0,1:T(8,128)S(1)}, u32[]{:S(2)}, u32[]{:S(2)}) collective-permute-start(f32[160,64]{0,1:T(8,128)S(1)} %get-tuple-element.45), channel_id=1, source_target_pairs={{0,16},{2,18},{4,20},{6,22},{8,24},{10,26},{12,28},{14,30},{16,0},... | collective-permute-start | bytes 122888 | tf_op jit(solution)/shard_map/ppermute | solution.py:103
  33.2 3.1 %collective-permute-start.6 = (f32[160,64]{0,1:T(8,128)S(1)}, f32[160,64]{0,1:T(8,128)S(1)}, u32[]{:S(2)}, u32[]{:S(2)}) collective-permute-start(f32[160,64]{0,1:T(8,128)S(1)} %get-tuple-element.44), channel_id=1, source_target_pairs={{0,8},{2,10},{4,12},{6,14},{8,0},{10,2},{12,4},{14,6},{16,24},{18,... | collective-permute-start | bytes 122888 | tf_op jit(solution)/shard_map/ppermute | solution.py:103
  36.3 0.9 %convolution_multiply_fusion = f32[96,64]{0,1:T(8,128)} fusion(f32[64,64]{1,0:T(8,128)S(1)} %copy-done, f32[160,64]{0,1:T(8,128)S(1)} %collective-permute-done.3, f32[192,64]{0,1:T(8,128)S(1)} %fusion.19, s32[]{:T(128)S(6)} %select_n.72), kind=kOutput, calls=%fused_computation.3 | convolution fusion | flops 4730880 | bytes 122884 | tf_op jit(solution)/shard_map/dot_general | solution.py:115
  37.2 0.9 %collective-permute-done.8 = f32[160,64]{0,1:T(8,128)S(1)} collective-permute-done((f32[160,64]{0,1:T(8,128)S(1)}, f32[160,64]{0,1:T(8,128)S(1)}, u32[]{:S(2)}, u32[]{:S(2)}) %collective-permute-start.8) | collective-permute-done | bytes 40992 | tf_op jit(solution)/shard_map/ppermute | solution.py:103
  38.1 1.1 %collective-permute-done.7 = f32[160,64]{0,1:T(8,128)S(1)} collective-permute-done((f32[160,64]{0,1:T(8,128)S(1)}, f32[160,64]{0,1:T(8,128)S(1)}, u32[]{:S(2)}, u32[]{:S(2)}) %collective-permute-start.7) | collective-permute-done | bytes 40992 | tf_op jit(solution)/shard_map/ppermute | solution.py:103
  39.2 0.0 collective-permute-done.6
  39.2 0.7 %fusion.8 = f32[64,64]{1,0:T(8,128)} fusion(f32[160,64]{0,1:T(8,128)S(1)} %collective-permute-done.8, f32[160,64]{0,1:T(8,128)S(1)} %collective-permute-done.7, f32[64,64]{0,1:T(8,128)S(1)} %fusion.10, f32[160,64]{0,1:T(8,128)S(1)} %collective-permute-done.6), kind=kLoop, calls=%fused_computation.22 | loop fusion | flops 16384 | bytes 81920 | tf_op jit(solution)/shard_map/mul | solution.py:117
  39.9 0.6 %fusion.9 = f32[96,64]{0,1:T(8,128)} fusion(f32[160,64]{0,1:T(8,128)S(1)} %collective-permute-done.8, f32[160,64]{0,1:T(8,128)S(1)} %collective-permute-done.7, f32[160,64]{0,1:T(8,128)S(1)} %collective-permute-done.6, f32[4,96,64]{1,2,0:T(8,128)S(1)} %fusion.5, s32[]{:T(128)S(6)} %select_n.109, pred[]{:T(512)S(6)} %and.58), kind=kLoop, calls=%fused_computation.25 | loop fusion | flops 30720 | bytes 122885 | tf_op jit(solution)/shard_map/mul | solution.py:116
  (9 shorter events, 0.1 us)
Async XLA Ops:
  0.6 16.1 %copy-start = (f32[64,64]{1,0:T(8,128)S(1)}, f32[64,64]{1,0:T(8,128)}, u32[]{:S(2)}) copy-start(f32[64,64]{1,0:T(8,128)} %param.13) | copy-start | bytes 49156
  0.6 18.1 %copy-start.2 = (s32[192,1536]{1,0:T(8,128)S(1)}, s32[192,1536]{1,0:T(8,128)}, u32[]{:S(2)}) copy-start(s32[192,1536]{1,0:T(8,128)} %param.10) | copy-start | bytes 3538948
  2.1 14.6 %all-to-all-start = ((bf16[8,96,64]{1,2,0:T(8,128)(2,1)}), bf16[8,96,64]{1,2,0:T(8,128)(2,1)S(1)}, u32[]{:S(2)}, u32[]{:S(2)}) async-start(bf16[8,96,64]{1,2,0:T(8,128)(2,1)} %broadcast_in_dim.33), calls=%async_computation | async-start | bytes 262144 | tf_op jit(solution)/shard_map/all_to_all | solution.py:50
  9.4 7.3 %collective-permute-start = (bf16[96,64]{0,1:T(8,128)(2,1)}, bf16[96,64]{0,1:T(8,128)(2,1)S(1)}, u32[]{:S(2)}, u32[]{:S(2)}) collective-permute-start(bf16[96,64]{0,1:T(8,128)(2,1)} %param.11), channel_id=1, source_target_pairs={{0,1},{1,0},{2,3},{3,2},{4,5},{5,4},{6,7},{7,6},{8,9},{9,8},{10,11... | collective-permute-start | bytes 36872 | tf_op jit(solution)/shard_map/ppermute | solution.py:44
  16.7 1.3 %collective-permute-start.1 = (bf16[8,96,64]{1,2,0:T(8,128)(2,1)S(1)}, bf16[8,96,64]{1,2,0:T(8,128)(2,1)S(1)}, u32[]{:S(2)}, u32[]{:S(2)}) collective-permute-start(bf16[8,96,64]{1,2,0:T(8,128)(2,1)S(1)} %all-to-all-done), channel_id=1, source_target_pairs={{0,2},{2,0},{1,3},{3,1},{4,6},{6,4},{5,7},{7,5},{8,10},{10,8},{9,1... | collective-permute-start | bytes 294920 | tf_op jit(solution)/shard_map/ppermute | solution.py:51
  20.7 0.7 %copy-start.1 = (bf16[96,64]{0,1:T(8,128)(2,1)S(1)}, bf16[96,64]{0,1:T(8,128)(2,1)}, u32[]{:S(2)}) copy-start(bf16[96,64]{0,1:T(8,128)(2,1)} %param.11) | copy-start | bytes 36868
  21.7 1.6 %collective-permute-start.2 = (f32[832,64]{0,1:T(8,128)S(1)}, f32[832,64]{0,1:T(8,128)S(1)}, u32[]{:S(2)}, u32[]{:S(2)}) collective-permute-start(f32[832,64]{0,1:T(8,128)S(1)} %pad_maximum_fusion), channel_id=1, source_target_pairs={{0,2},{2,0},{4,6},{6,4},{8,10},{10,8},{12,14},{14,12},{16,18},{18,... | collective-permute-start | bytes 638984 | tf_op jit(solution)/shard_map/ppermute | solution.py:85
  23.8 6.1 %collective-permute-start.4 = (f32[448,64]{0,1:T(8,128)S(1)}, f32[448,64]{0,1:T(8,128)S(1)}, u32[]{:S(2)}, u32[]{:S(2)}) collective-permute-start(f32[448,64]{0,1:T(8,128)S(1)} %pad_maximum_fusion.1), channel_id=1, source_target_pairs={{0,4},{2,6},{4,0},{6,2},{8,12},{10,14},{12,8},{14,10},{16,20},{18,... | collective-permute-start | bytes 344072 | tf_op jit(solution)/shard_map/ppermute | solution.py:85
  24.1 7.1 %collective-permute-start.5 = (f32[64,64]{0,1:T(8,128)S(1)}, f32[64,64]{0,1:T(8,128)S(1)}, u32[]{:S(2)}, u32[]{:S(2)}) collective-permute-start(f32[64,64]{0,1:T(8,128)S(1)} %slice_add_fusion.9), channel_id=1, source_target_pairs={{0,5},{1,4},{2,7},{3,6},{4,1},{5,0},{6,3},{7,2},{8,13},{9,12},{10,... | collective-permute-start | bytes 49160 | tf_op jit(solution)/shard_map/ppermute | solution.py:90
  27.0 4.7 %collective-permute-start.3 = (f32[160,64]{0,1:T(8,128)S(1)}, f32[160,64]{0,1:T(8,128)S(1)}, u32[]{:S(2)}, u32[]{:S(2)}) collective-permute-start(f32[160,64]{0,1:T(8,128)S(1)} %pad_maximum_fusion.5), channel_id=1, source_target_pairs={{0,1},{1,0},{2,3},{3,2},{4,5},{5,4},{6,7},{7,6},{8,9},{9,8},{10,11... | collective-permute-start | bytes 122888 | tf_op jit(solution)/shard_map/ppermute | solution.py:89
  31.9 6.3 %collective-permute-start.8 = (f32[160,64]{0,1:T(8,128)S(1)}, f32[160,64]{0,1:T(8,128)S(1)}, u32[]{:S(2)}, u32[]{:S(2)}) collective-permute-start(f32[160,64]{0,1:T(8,128)S(1)} %get-tuple-element.46), channel_id=1, source_target_pairs={{0,24},{2,26},{4,28},{6,30},{8,16},{10,18},{12,20},{14,22},{16,8},... | collective-permute-start | bytes 122888 | tf_op jit(solution)/shard_map/ppermute | solution.py:103
  32.5 6.7 %collective-permute-start.7 = (f32[160,64]{0,1:T(8,128)S(1)}, f32[160,64]{0,1:T(8,128)S(1)}, u32[]{:S(2)}, u32[]{:S(2)}) collective-permute-start(f32[160,64]{0,1:T(8,128)S(1)} %get-tuple-element.45), channel_id=1, source_target_pairs={{0,16},{2,18},{4,20},{6,22},{8,24},{10,26},{12,28},{14,30},{16,0},... | collective-permute-start | bytes 122888 | tf_op jit(solution)/shard_map/ppermute | solution.py:103
  33.2 6.0 %collective-permute-start.6 = (f32[160,64]{0,1:T(8,128)S(1)}, f32[160,64]{0,1:T(8,128)S(1)}, u32[]{:S(2)}, u32[]{:S(2)}) collective-permute-start(f32[160,64]{0,1:T(8,128)S(1)} %get-tuple-element.44), channel_id=1, source_target_pairs={{0,8},{2,10},{4,12},{6,14},{8,0},{10,2},{12,4},{14,6},{16,24},{18,... | collective-permute-start | bytes 122888 | tf_op jit(solution)/shard_map/ppermute | solution.py:103

commit v7 on v6

--- a/solution.py
+++ b/solution.py
@@ -49,8 +49,18 @@
     core = lax.axis_index("core")
     by_chip = lax.all_to_all(jnp.broadcast_to(phi[None], (nchip,) + phi.shape), "chip", 0, 0)
     other = lax.ppermute(by_chip, "core", SWAP)
-    pair = jnp.where(core == 0, jnp.stack([by_chip, other], axis=1), jnp.stack([other, by_chip], axis=1))
-    members = pair.reshape(nr * phi.shape[0], k)
+    mr = phi.shape[0]
+    special = nc == 2 and nr == 16
+    if special:
+        def xz(a):
+            return jnp.swapaxes(a.reshape(4, 2, mr, k), 0, 1).reshape(8 * mr, k)
+        members = jnp.where(core == 0, jnp.concatenate([xz(by_chip), xz(other)]),
+                            jnp.concatenate([xz(other), xz(by_chip)]))
+        rows = counts.shape[0]
+        counts = jnp.transpose(counts.reshape(rows, 4, 2, 2, mr), (0, 3, 2, 1, 4)).reshape(rows, 16 * mr)
+    else:
+        pair = jnp.where(core == 0, jnp.stack([by_chip, other], axis=1), jnp.stack([other, by_chip], axis=1))
+        members = pair.reshape(nr * phi.shape[0], k)
     theta_wide = theta_rows.astype(jnp.float32)
     row_factor = jnp.dot(theta_wide, affinity, precision=HI)
     factor_half = row_factor.astype(jnp.bfloat16)
@@ -76,6 +86,24 @@
     mr = gcol.shape[0] // nr
     acc = gcol.reshape(nr, mr, k)
     b = 1
+    if special:
+        half = 8 * mr
+        got = lax.ppermute(jnp.concatenate([lax.dynamic_slice_in_dim(gcol, (1 - core) * half, half), part_sum]),
+                           ROW, [(i, i ^ 1) for i in range(nr)])
+        acc = lax.dynamic_slice_in_dim(gcol, core * half, half) + got[:half]
+        part_sum = part_sum + got[half:]
+        x = (r // 2) % 2
+        half = 4 * mr
+        got = lax.ppermute(jnp.concatenate([lax.dynamic_slice_in_dim(acc, (1 - x) * half, half), part_sum]),
+                           ROW, [(i, i ^ 2) for i in range(nr)])
+        send = jnp.concatenate([lax.dynamic_slice_in_dim(gphi, (1 - c) * mc, mc), part_sum])
+        got_col = lax.ppermute(send, "col", SWAP)
+        got_diag = lax.ppermute(part_sum, ROW + ("col",), [(i, i ^ 5) for i in range(nr * nc)])
+        gphi_sum = lax.dynamic_slice_in_dim(gphi, c * mc, mc) + got_col[:mc]
+        acc = (lax.dynamic_slice_in_dim(acc, x * half, half) + got[:half]).reshape(4, mr, k)
+        part_sum = (part_sum + got_col[mc:]) + (got[half:] + got_diag)
+        b = 4
+        deferred = False
     while b < nr // 4:
         pairs = acc.reshape(acc.shape[0] // 2, 2, mr, k)
         mine = (r // b) % 2

time: 41.2 us -> 39.5 us (0.959)
  waiting for transfers between devices: 13.3 us -> 8.87 us
  local copies, waits for them, and re-layouts: 3.93 us -> 6.63 us
  other arithmetic: 1.91 us -> 3.04 us
  matrix products: 3.4 us -> 2.59 us
    all_to_all x1, waiting for transfers between devices: 5.82 us -> 0.05 us  [shards(): lax.all_to_all(jnp.broadcast_to(phi[None], (nchip,) + phi.shape), 'chip',...]
    convert_element_type x0 -> x3, local copies, waits for them, and re-layouts: none -> 4.38 us  [shards(): ratio = (1.0 - counts.astype(jnp.float32) / rate).astype(jnp.bfloat16)]
    convert_element_type x0 -> x1, other arithmetic: none -> 1.36 us  [shards(): ratio = (1.0 - counts.astype(jnp.float32) / rate).astype(jnp.bfloat16)]
    another operation x2 -> x1, local copies, waits for them, and re-layouts: 1.12 us -> 0.12 us  [shards(): total = jnp.take(acc, quad, axis=0)]
    ppermute x3, waiting for transfers between devices: 2.07 us -> 2.93 us  [shards(): got = lax.ppermute(send, ROW, [(i, i ^ s * b) for i in range(nr)])]
    dot_general x1, matrix products: 1.06 us -> 0.26 us  [shards(): row_factor = jnp.dot(theta_wide, affinity, precision=HI)]
    select_n x3 -> x0, local copies, waits for them, and re-layouts: 0.62 us -> none  [the longest x2 0.53 us: shards(): jnp.where(core == 0, jnp.stack([by_chip, other], axis=1), jnp.stack([othe...]
    ppermute x1, waiting for transfers between devices: 0.27 us -> 0.78 us  [shards(): other = lax.ppermute(by_chip, 'core', SWAP)]
  transfers between devices with their start and end apart: 10 -> 10, of which waited for: 8 -> 8; matrix products, arithmetic and copies ran while one was open for 6% -> 19% of each run, Pallas kernels for 0% -> 0%
where the time goes in v7:
time: 39.5 us; the launch traced here: 39.1 us
  starting transfers between devices  17.1 us (43%)
  waiting for transfers between devices  8.87 us (22%)
  local copies, waits for them, and re-layouts  6.63 us (17%)
  other arithmetic  3.04 us (8%)
  matrix products  2.59 us (7%)
  between operations  0.85 us (2%)
    all_to_all x1, starting transfers between devices, shards(): lax.all_to_all(jnp.broadcast_to(phi[None], (nchip,) + phi.shape), 'chip',...  7.25 us
    ppermute x3, starting transfers between devices, shards(): got = lax.ppermute(send, ROW, [(i, i ^ s * b) for i in range(nr)])  4.45 us
    convert_element_type x3, local copies, waits for them, and re-layouts, shards(): ratio = (1.0 - counts.astype(jnp.float32) / rate).astype(jnp.bfloat16)  4.38 us
    ppermute x3, waiting for transfers between devices, shards(): got = lax.ppermute(send, ROW, [(i, i ^ s * b) for i in range(nr)])  2.93 us
    ppermute x1, waiting for transfers between devices, shards(): lax.ppermute(jnp.concatenate([lax.dynamic_slice_in_dim(acc, (1 - x) * hal...  2.44 us
    ppermute x1, starting transfers between devices, shards(): lax.ppermute(jnp.concatenate([lax.dynamic_slice_in_dim(acc, (1 - x) * hal...  2.08 us
    ppermute x1, starting transfers between devices, shards(): other = lax.ppermute(theta, 'col', SWAP)  1.52 us
    broadcast_in_dim x1, local copies, waits for them, and re-layouts, shards(): jnp.broadcast_to(phi[None], (nchip,) + phi.shape)  1.4 us
  transfers between devices with their start and end apart: 10, of which 8 were waited for; matrix products, arithmetic and copies ran while one was open for 19% of the time, Pallas kernels for 0%

profile of v7, /device:TPU:0, one launch (start us, length us, event | category | flops | bytes accessed | tf_op | source)
XLA Modules:
  0.0 39.1 jit_solution(1351846264628270411)
XLA Ops:
  0.6 0.0 copy-start
  0.6 1.4 %broadcast_in_dim.15 = bf16[8,96,64]{1,2,0:T(8,128)(2,1)} broadcast(bf16[96,64]{0,1:T(8,128)(2,1)} %param.8), dimensions={1,2} | broadcast | bytes 110592 | tf_op jit(solution)/shard_map/broadcast_in_dim | solution.py:50
  2.0 7.3 %all-to-all-start = ((bf16[8,96,64]{1,2,0:T(8,128)(2,1)}), bf16[8,96,64]{1,2,0:T(8,128)(2,1)S(1)}, u32[]{:S(2)}, u32[]{:S(2)}) async-start(bf16[8,96,64]{1,2,0:T(8,128)(2,1)} %broadcast_in_dim.15), calls=%async_computation | async-start | bytes 262144 | tf_op jit(solution)/shard_map/all_to_all | solution.py:50
  9.3 1.5 %collective-permute-start = (bf16[96,64]{0,1:T(8,128)(2,1)}, bf16[96,64]{0,1:T(8,128)(2,1)S(1)}, u32[]{:S(2)}, u32[]{:S(2)}) collective-permute-start(bf16[96,64]{0,1:T(8,128)(2,1)} %param.7), channel_id=1, source_target_pairs={{0,1},{1,0},{2,3},{3,2},{4,5},{5,4},{6,7},{7,6},{8,9},{9,8},{10,11... | collective-permute-start | bytes 36872 | tf_op jit(solution)/shard_map/ppermute | solution.py:44
  10.8 1.4 %convert_element_type.20 = f32[192,1536]{1,0:T(8,128)S(1)} convert(s32[192,1536]{1,0:T(8,128)} %param.6) | non-fusion elementwise | flops 294912 | bytes 2359296 | tf_op jit(solution)/shard_map/convert_element_type | solution.py:68
  12.2 2.4 %convert_element_type.21 = f32[192,4,2,2,96]{4,3,2,1,0:T(2,128)S(1)} reshape(f32[192,1536]{1,0:T(8,128)S(1)} %convert_element_type.20) | data formatting | bytes 2359296 | tf_op jit(solution)/shard_map/convert_element_type | solution.py:68
  14.6 0.4 %copy.26 = f32[192,4,2,2,96]{4,1,2,3,0:T(4,128)S(1)} copy(f32[192,4,2,2,96]{4,3,2,1,0:T(2,128)S(1)} %convert_element_type.21) | data formatting | bytes 2359296 | tf_op jit(solution)/shard_map/convert_element_type | solution.py:68
  15.0 0.0 copy-start.1
  15.0 1.6 %convert_element_type.23 = f32[192,1536]{1,0:T(8,128)S(1)} reshape(f32[192,2,2,4,96]{4,3,2,1,0:T(4,128)S(1)} %bitcast.35) | data formatting | bytes 2359296 | tf_op jit(solution)/shard_map/convert_element_type | solution.py:68
  16.6 0.1 all-to-all-done
  16.6 0.0 collective-permute-start.1
  16.7 0.0 collective-permute-done
  16.7 0.0 copy-done
  16.7 0.0 copy-done.1
  16.7 0.3 fusion.12
  17.0 0.1 copy.15
  17.1 0.1 reshape.32
  17.2 0.8 %collective-permute-done.1 = bf16[8,96,64]{1,2,0:T(8,128)(2,1)S(1)} collective-permute-done((bf16[8,96,64]{1,2,0:T(8,128)(2,1)S(1)}, bf16[8,96,64]{1,2,0:T(8,128)(2,1)S(1)}, u32[]{:S(2)}, u32[]{:S(2)}) %collective-permute-start.1) | collective-permute-done | bytes 98336 | tf_op jit(solution)/shard_map/ppermute | solution.py:51
  18.0 0.1 copy.16
  18.1 0.1 reshape.34
  18.3 0.7 %fusion.1 = bf16[192,1536]{1,0:T(8,128)(2,1)S(1)} fusion(f32[192,1536]{1,0:T(8,128)S(1)} %convert_element_type.23, f32[192,64]{0,1:T(8,128)S(1)} %fusion.12, bf16[768,64]{0,1:T(8,128)(2,1)S(1)} %reshape.34, bf16[768,64]{0,1:T(8,128)(2,1)S(1)} %reshape.32, pred[]{:T(512)S(6)} %eq.10), kind=kOutput, calls=%fused_computation.2 | convolution fusion | flops 228261888 | bytes 2015233 | tf_op jit(solution)/shard_map/dot_general | solution.py:67
  19.0 0.3 fusion.2
  19.3 0.2 fusion.8
  19.5 0.2 fusion.11
  19.8 0.2 collective-permute-start.2
  20.0 1.3 %collective-permute-done.2 = f32[832,64]{0,1:T(8,128)S(1)} collective-permute-done((f32[832,64]{0,1:T(8,128)S(1)}, f32[832,64]{0,1:T(8,128)S(1)}, u32[]{:S(2)}, u32[]{:S(2)}) %collective-permute-start.2) | collective-permute-done | bytes 213024 | tf_op jit(solution)/shard_map/ppermute | solution.py:91
  21.5 2.1 %collective-permute-start.4 = (f32[448,64]{0,1:T(8,128)S(1)}, f32[448,64]{0,1:T(8,128)S(1)}, u32[]{:S(2)}, u32[]{:S(2)}) collective-permute-start(f32[448,64]{0,1:T(8,128)S(1)} %pad_maximum_fusion.1), channel_id=1, source_target_pairs={{0,4},{2,6},{4,0},{6,2},{8,12},{10,14},{12,8},{14,10},{16,20},{18,... | collective-permute-start | bytes 344072 | tf_op jit(solution)/shard_map/ppermute | solution.py:97
  23.5 0.1 constant_dynamic-slice_fusion.6
  23.6 1.0 %collective-permute-start.5 = (f32[64,64]{0,1:T(8,128)S(1)}, f32[64,64]{0,1:T(8,128)S(1)}, u32[]{:S(2)}, u32[]{:S(2)}) collective-permute-start(f32[64,64]{0,1:T(8,128)S(1)} %slice_add_fusion.11), channel_id=1, source_target_pairs={{0,5},{1,4},{2,7},{3,6},{4,1},{5,0},{6,3},{7,2},{8,13},{9,12},{10,... | collective-permute-start | bytes 49160 | tf_op jit(solution)/shard_map/ppermute | solution.py:101
  24.6 0.1 pad_maximum_fusion.5
  24.7 0.6 %collective-permute-start.3 = (f32[160,64]{0,1:T(8,128)S(1)}, f32[160,64]{0,1:T(8,128)S(1)}, u32[]{:S(2)}, u32[]{:S(2)}) collective-permute-start(f32[160,64]{0,1:T(8,128)S(1)} %pad_maximum_fusion.5), channel_id=1, source_target_pairs={{0,1},{1,0},{2,3},{3,2},{4,5},{5,4},{6,7},{7,6},{8,9},{9,8},{10,11... | collective-permute-start | bytes 122888 | tf_op jit(solution)/shard_map/ppermute | solution.py:100
  25.3 2.4 %collective-permute-done.4 = f32[448,64]{0,1:T(8,128)S(1)} collective-permute-done((f32[448,64]{0,1:T(8,128)S(1)}, f32[448,64]{0,1:T(8,128)S(1)}, u32[]{:S(2)}, u32[]{:S(2)}) %collective-permute-start.4) | collective-permute-done | bytes 114720 | tf_op jit(solution)/shard_map/ppermute | solution.py:97
  27.7 0.1 reshape.35
  27.8 0.1 constant_dynamic-slice_fusion.3
  28.0 0.8 %collective-permute-done.5 = f32[64,64]{0,1:T(8,128)S(1)} collective-permute-done((f32[64,64]{0,1:T(8,128)S(1)}, f32[64,64]{0,1:T(8,128)S(1)}, u32[]{:S(2)}, u32[]{:S(2)}) %collective-permute-start.5) | collective-permute-done | bytes 16416 | tf_op jit(solution)/shard_map/ppermute | solution.py:101
  28.8 0.5 %collective-permute-done.3 = f32[160,64]{0,1:T(8,128)S(1)} collective-permute-done((f32[160,64]{0,1:T(8,128)S(1)}, f32[160,64]{0,1:T(8,128)S(1)}, u32[]{:S(2)}, u32[]{:S(2)}) %collective-permute-start.3) | collective-permute-done | bytes 40992 | tf_op jit(solution)/shard_map/ppermute | solution.py:100
  29.3 0.1 fusion.7
  29.4 0.1 pad_maximum_fusion.4
  29.5 2.9 %collective-permute-start.8 = (f32[160,64]{0,1:T(8,128)S(1)}, f32[160,64]{0,1:T(8,128)S(1)}, u32[]{:S(2)}, u32[]{:S(2)}) collective-permute-start(f32[160,64]{0,1:T(8,128)S(1)} %get-tuple-element.21), channel_id=1, source_target_pairs={{0,24},{2,26},{4,28},{6,30},{8,16},{10,18},{12,20},{14,22},{16,8},... | collective-permute-start | bytes 122888 | tf_op jit(solution)/shard_map/ppermute | solution.py:131
  32.4 0.0 collective-permute-start.7
  32.4 1.6 %collective-permute-start.6 = (f32[160,64]{0,1:T(8,128)S(1)}, f32[160,64]{0,1:T(8,128)S(1)}, u32[]{:S(2)}, u32[]{:S(2)}) collective-permute-start(f32[160,64]{0,1:T(8,128)S(1)} %get-tuple-element.19), channel_id=1, source_target_pairs={{0,8},{2,10},{4,12},{6,14},{8,0},{10,2},{12,4},{14,6},{16,24},{18,... | collective-permute-start | bytes 122888 | tf_op jit(solution)/shard_map/ppermute | solution.py:131
  34.0 0.9 %convolution_multiply_fusion = f32[96,64]{0,1:T(8,128)} fusion(f32[64,64]{1,0:T(8,128)S(1)} %copy-done, f32[160,64]{0,1:T(8,128)S(1)} %collective-permute-done.3, f32[192,64]{0,1:T(8,128)S(1)} %fusion.2, s32[]{:T(128)S(6)} %select_n.62), kind=kOutput, calls=%fused_computation.4 | convolution fusion | flops 4730880 | bytes 122884 | tf_op jit(solution)/shard_map/dot_general | solution.py:143
  34.8 1.1 %collective-permute-done.8 = f32[160,64]{0,1:T(8,128)S(1)} collective-permute-done((f32[160,64]{0,1:T(8,128)S(1)}, f32[160,64]{0,1:T(8,128)S(1)}, u32[]{:S(2)}, u32[]{:S(2)}) %collective-permute-start.8) | collective-permute-done | bytes 40992 | tf_op jit(solution)/shard_map/ppermute | solution.py:131
  35.9 1.9 %collective-permute-done.7 = f32[160,64]{0,1:T(8,128)S(1)} collective-permute-done((f32[160,64]{0,1:T(8,128)S(1)}, f32[160,64]{0,1:T(8,128)S(1)}, u32[]{:S(2)}, u32[]{:S(2)}) %collective-permute-start.7) | collective-permute-done | bytes 40992 | tf_op jit(solution)/shard_map/ppermute | solution.py:131
  37.7 0.0 collective-permute-done.6
  37.8 0.7 %fusion.5 = f32[64,64]{1,0:T(8,128)} fusion(f32[160,64]{0,1:T(8,128)S(1)} %collective-permute-done.8, f32[160,64]{0,1:T(8,128)S(1)} %collective-permute-done.7, f32[64,64]{0,1:T(8,128)S(1)} %fusion.7, f32[160,64]{0,1:T(8,128)S(1)} %collective-permute-done.6), kind=kLoop, calls=%fused_computation.18 | loop fusion | flops 16384 | bytes 81920 | tf_op jit(solution)/shard_map/mul | solution.py:145
  38.5 0.6 %fusion.6 = f32[96,64]{0,1:T(8,128)} fusion(f32[160,64]{0,1:T(8,128)S(1)} %collective-permute-done.8, f32[160,64]{0,1:T(8,128)S(1)} %collective-permute-done.7, f32[160,64]{0,1:T(8,128)S(1)} %collective-permute-done.6, f32[1,96,64]{1,2,0:T(8,128)S(1)} %bitcast.38, pred[]{:T(512)S(6)} %and.35), kind=kLoop, calls=%fused_computation.21 | loop fusion | flops 30720 | bytes 122881 | tf_op jit(solution)/shard_map/mul | solution.py:144
  (9 shorter events, 0.1 us)
Async XLA Ops:
  0.6 16.1 %copy-start = (f32[64,64]{1,0:T(8,128)S(1)}, f32[64,64]{1,0:T(8,128)}, u32[]{:S(2)}) copy-start(f32[64,64]{1,0:T(8,128)} %param.9) | copy-start | bytes 49156
  2.0 14.6 %all-to-all-start = ((bf16[8,96,64]{1,2,0:T(8,128)(2,1)}), bf16[8,96,64]{1,2,0:T(8,128)(2,1)S(1)}, u32[]{:S(2)}, u32[]{:S(2)}) async-start(bf16[8,96,64]{1,2,0:T(8,128)(2,1)} %broadcast_in_dim.15), calls=%async_computation | async-start | bytes 262144 | tf_op jit(solution)/shard_map/all_to_all | solution.py:50
  9.3 7.4 %collective-permute-start = (bf16[96,64]{0,1:T(8,128)(2,1)}, bf16[96,64]{0,1:T(8,128)(2,1)S(1)}, u32[]{:S(2)}, u32[]{:S(2)}) collective-permute-start(bf16[96,64]{0,1:T(8,128)(2,1)} %param.7), channel_id=1, source_target_pairs={{0,1},{1,0},{2,3},{3,2},{4,5},{5,4},{6,7},{7,6},{8,9},{9,8},{10,11... | collective-permute-start | bytes 36872 | tf_op jit(solution)/shard_map/ppermute | solution.py:44
  15.0 1.7 %copy-start.1 = (bf16[96,64]{0,1:T(8,128)(2,1)S(1)}, bf16[96,64]{0,1:T(8,128)(2,1)}, u32[]{:S(2)}) copy-start(bf16[96,64]{0,1:T(8,128)(2,1)} %param.7) | copy-start | bytes 36868
  16.6 1.4 %collective-permute-start.1 = (bf16[8,96,64]{1,2,0:T(8,128)(2,1)S(1)}, bf16[8,96,64]{1,2,0:T(8,128)(2,1)S(1)}, u32[]{:S(2)}, u32[]{:S(2)}) collective-permute-start(bf16[8,96,64]{1,2,0:T(8,128)(2,1)S(1)} %all-to-all-done), channel_id=1, source_target_pairs={{0,2},{2,0},{1,3},{3,1},{4,6},{6,4},{5,7},{7,5},{8,10},{10,8},{9,1... | collective-permute-start | bytes 294920 | tf_op jit(solution)/shard_map/ppermute | solution.py:51
  19.8 1.6 %collective-permute-start.2 = (f32[832,64]{0,1:T(8,128)S(1)}, f32[832,64]{0,1:T(8,128)S(1)}, u32[]{:S(2)}, u32[]{:S(2)}) collective-permute-start(f32[832,64]{0,1:T(8,128)S(1)} %pad_maximum_fusion), channel_id=1, source_target_pairs={{0,2},{2,0},{4,6},{6,4},{8,10},{10,8},{12,14},{14,12},{16,18},{18,... | collective-permute-start | bytes 638984 | tf_op jit(solution)/shard_map/ppermute | solution.py:91
  21.5 6.2 %collective-permute-start.4 = (f32[448,64]{0,1:T(8,128)S(1)}, f32[448,64]{0,1:T(8,128)S(1)}, u32[]{:S(2)}, u32[]{:S(2)}) collective-permute-start(f32[448,64]{0,1:T(8,128)S(1)} %pad_maximum_fusion.1), channel_id=1, source_target_pairs={{0,4},{2,6},{4,0},{6,2},{8,12},{10,14},{12,8},{14,10},{16,20},{18,... | collective-permute-start | bytes 344072 | tf_op jit(solution)/shard_map/ppermute | solution.py:97
  23.6 5.2 %collective-permute-start.5 = (f32[64,64]{0,1:T(8,128)S(1)}, f32[64,64]{0,1:T(8,128)S(1)}, u32[]{:S(2)}, u32[]{:S(2)}) collective-permute-start(f32[64,64]{0,1:T(8,128)S(1)} %slice_add_fusion.11), channel_id=1, source_target_pairs={{0,5},{1,4},{2,7},{3,6},{4,1},{5,0},{6,3},{7,2},{8,13},{9,12},{10,... | collective-permute-start | bytes 49160 | tf_op jit(solution)/shard_map/ppermute | solution.py:101
  24.7 4.7 %collective-permute-start.3 = (f32[160,64]{0,1:T(8,128)S(1)}, f32[160,64]{0,1:T(8,128)S(1)}, u32[]{:S(2)}, u32[]{:S(2)}) collective-permute-start(f32[160,64]{0,1:T(8,128)S(1)} %pad_maximum_fusion.5), channel_id=1, source_target_pairs={{0,1},{1,0},{2,3},{3,2},{4,5},{5,4},{6,7},{7,6},{8,9},{9,8},{10,11... | collective-permute-start | bytes 122888 | tf_op jit(solution)/shard_map/ppermute | solution.py:100
  29.5 6.4 %collective-permute-start.8 = (f32[160,64]{0,1:T(8,128)S(1)}, f32[160,64]{0,1:T(8,128)S(1)}, u32[]{:S(2)}, u32[]{:S(2)}) collective-permute-start(f32[160,64]{0,1:T(8,128)S(1)} %get-tuple-element.21), channel_id=1, source_target_pairs={{0,24},{2,26},{4,28},{6,30},{8,16},{10,18},{12,20},{14,22},{16,8},... | collective-permute-start | bytes 122888 | tf_op jit(solution)/shard_map/ppermute | solution.py:131
  32.4 5.3 %collective-permute-start.7 = (f32[160,64]{0,1:T(8,128)S(1)}, f32[160,64]{0,1:T(8,128)S(1)}, u32[]{:S(2)}, u32[]{:S(2)}) collective-permute-start(f32[160,64]{0,1:T(8,128)S(1)} %get-tuple-element.20), channel_id=1, source_target_pairs={{0,16},{2,18},{4,20},{6,22},{8,24},{10,26},{12,28},{14,30},{16,0},... | collective-permute-start | bytes 122888 | tf_op jit(solution)/shard_map/ppermute | solution.py:131
  32.4 5.3 %collective-permute-start.6 = (f32[160,64]{0,1:T(8,128)S(1)}, f32[160,64]{0,1:T(8,128)S(1)}, u32[]{:S(2)}, u32[]{:S(2)}) collective-permute-start(f32[160,64]{0,1:T(8,128)S(1)} %get-tuple-element.19), channel_id=1, source_target_pairs={{0,8},{2,10},{4,12},{6,14},{8,0},{10,2},{12,4},{14,6},{16,24},{18,... | collective-permute-start | bytes 122888 | tf_op jit(solution)/shard_map/ppermute | solution.py:131
